TPU v7x, 32 devices: a whole 2x2x4 slice. The times are simulated.
32 devices in a mesh: ctx: 16 (over z, y, x), tp: 2 (over core).
Axes of the slice: x: 2, y: 2, z: 4, core: 2. Of those that a mesh axis runs over, the one named last changes fastest.
Arguments:
- x_act: bfloat16 [4096, 8192], P('ctx', 'tp'), may hold values from -0.119628906 to 0.119628906
- b_proj: bfloat16 [4096, 128], P('ctx'), may hold values from -0.5 to 0.5
- c_proj: bfloat16 [4096, 128], P('ctx'), may hold values from -0.5 to 0.5
- dt_raw: bfloat16 [4096, 128], P('ctx', 'tp'), may hold values from -3 to 3
- a_log: float32 [128], P('tp'), may hold values from -12 to -2
- d_skip: float32 [128], P('tp'), may hold values from 0.5 to 2
- grad_out: bfloat16 [4096, 8192], P('ctx', 'tp'), may hold values from -6 to 6
Outputs:
- grad_x: bfloat16 [4096, 8192], P('ctx', 'tp')
- grad_b: float32 [4096, 128], P('ctx')
- grad_c: float32 [4096, 128], P('ctx')
- grad_dt: bfloat16 [4096, 128], P('ctx', 'tp')
All inputs are finite; a program needn't handle non-finite values.
Results may differ from a plain program's by a relative error of at most 0.001.
Values may be sent and summed in bfloat16 or wider, within the bound.
No kernel may reach another device: no remote copies, remote signals or barrier semaphores. Data moves between devices by JAX's collectives and lax.ppermute only.
A program may use at most 192 MiB of HBM per device.

v0:
```python
from functools import partial

import jax
import jax.numpy as jnp
from jax import lax
from jax.sharding import PartitionSpec as P

BLOCK = 256


precise = lax.Precision.HIGH


def head_forward(x_head, b_rows, c_rows, raw_step, log_rate, skip_gain, start_state, block_len):
    length, head_width = x_head.shape
    blocks = length // block_len
    step_size = jax.nn.softplus(raw_step)
    decay_rates = -jnp.exp(log_rate) * step_size
    row_index = lax.broadcasted_iota(jnp.int32, (block_len, block_len), 0)
    col_index = lax.broadcasted_iota(jnp.int32, (block_len, block_len), 1)
    lower_mask = row_index >= col_index
    running = jnp.dot(
        decay_rates.reshape(blocks, block_len), lower_mask.astype(jnp.float32).T, precision=precise
    )
    between = jnp.where(lower_mask[None], running[:, :, None] - running[:, None, :], -1e30)
    x_blocks = x_head.reshape(blocks, block_len, head_width)
    b_blocks = b_rows.reshape(blocks, block_len, -1)
    c_blocks = c_rows.reshape(blocks, block_len, -1)
    s_blocks = step_size.reshape(blocks, block_len)
    scores = (
        jnp.einsum("kin,kjn->kij", c_blocks, b_blocks, precision=precise)
        * jnp.exp(between)
        * s_blocks[:, None, :]
    )
    output = jnp.einsum("kij,kjp->kip", scores, x_blocks, precision=precise)
    closing = running[:, -1]
    weighted = (jnp.exp(closing[:, None] - running) * s_blocks)[:, :, None] * x_blocks
    states = jnp.einsum("kjp,kjn->kpn", weighted, b_blocks, precision=precise)
    block_rows = lax.broadcasted_iota(jnp.int32, (blocks, blocks), 0)
    block_cols = lax.broadcasted_iota(jnp.int32, (blocks, blocks), 1)
    through = jnp.dot((block_rows >= block_cols).astype(jnp.float32), closing, precision=precise)
    before = through - closing
    carry_weight = jnp.exp(
        jnp.where(block_rows > block_cols, before[:, None] - through[None, :], -1e30)
    )
    entering = (
        jnp.einsum("kj,jpn->kpn", carry_weight, states, precision=precise)
        + jnp.exp(before)[:, None, None] * start_state[None]
    )
    reading = jnp.exp(running)[:, :, None] * c_blocks
    output = output + jnp.einsum("kin,kpn->kip", reading, entering, precision=precise)
    output = output.reshape(length, head_width) + skip_gain * x_head
    final_state = (
        jnp.einsum("j,jpn->pn", jnp.exp(through[-1] - through), states, precision=precise)
        + jnp.exp(through[-1]) * start_state
    )
    return (output, final_state)


N_CHUNKS = 1


def chunk_backward(x_seq, g_seq, raw_seq, b_rows, c_rows, rate, gain):
    length = x_seq.shape[0]
    heads = raw_seq.shape[1]
    head_width = x_seq.shape[1] // heads
    runner = partial(head_forward, block_len=BLOCK)
    mapped = jax.vmap(runner, in_axes=(0, None, None, 0, 0, 0, 0))
    x_heads = x_seq.astype(jnp.float32).reshape(length, heads, head_width).transpose(1, 0, 2)
    g_heads = g_seq.astype(jnp.float32).reshape(length, heads, head_width).transpose(1, 0, 2)
    raw_heads = raw_seq.astype(jnp.float32).T
    anchor = jnp.zeros((heads, head_width, b_rows.shape[1]), jnp.float32)

    def forward(x_val, b_val, c_val, raw_val):
        return mapped(x_val, b_val, c_val, raw_val, rate, gain, anchor)[0]

    _, pullback = jax.vjp(forward, x_heads, b_rows, c_rows, raw_heads)
    grad_xh, grad_b_all, grad_c_all, grad_raw = pullback(g_heads)
    x_back = grad_xh.transpose(1, 0, 2).reshape(length, heads * head_width).astype(jnp.bfloat16)
    raw_back = grad_raw.T.astype(jnp.bfloat16)
    return x_back, raw_back, grad_b_all, grad_c_all


def gather_ctx(block, owners, me):
    if owners & (owners - 1):
        return lax.all_gather(block, "ctx", axis=0, tiled=True)
    have = block
    step = 1
    while step < owners:
        theirs = lax.ppermute(have, "ctx", [(k, k ^ step) for k in range(owners)])
        upper = (me // step) % 2 == 1
        have = jnp.where(upper, jnp.concatenate([theirs, have]), jnp.concatenate([have, theirs]))
        step *= 2
    return have


def local(x_act, b_proj, c_proj, dt_raw, a_log, d_skip, grad_out):
    rows = x_act.shape[0]
    heads_here = dt_raw.shape[1]
    head_width = x_act.shape[1] // heads_here
    state = b_proj.shape[1]
    owners = lax.axis_size("ctx")
    per_owner = heads_here // owners
    chunks = N_CHUNKS if per_owner % N_CHUNKS == 0 else 1
    per_chunk = per_owner // chunks
    me = lax.axis_index("ctx")
    half = lax.axis_index("tp")

    own_seq = gather_ctx(jnp.where(half == 0, b_proj, c_proj), owners, me)
    other_seq = lax.ppermute(own_seq, "tp", [(0, 1), (1, 0)])
    b_rows = jnp.where(half == 0, own_seq, other_seq).astype(jnp.float32)
    c_rows = jnp.where(half == 0, other_seq, own_seq).astype(jnp.float32)
    first_head = me * per_owner
    rate_own = lax.dynamic_slice_in_dim(a_log, first_head, per_owner)
    gain_own = lax.dynamic_slice_in_dim(d_skip, first_head, per_owner)

    x4 = x_act.reshape(rows, owners, per_owner, head_width)
    g4 = grad_out.reshape(rows, owners, per_owner, head_width)
    r3 = dt_raw.reshape(rows, owners, per_owner)
    x_parts, raw_parts = [], []
    grad_b_all = None
    grad_c_all = None
    for c in range(chunks):
        sl = slice(c * per_chunk, (c + 1) * per_chunk)
        width = per_chunk * head_width
        x_in = x4[:, :, sl, :].reshape(rows, owners, width)
        g_in = g4[:, :, sl, :].reshape(rows, owners, width)
        if c == 0:
            x_in, g_in, _ = lax.optimization_barrier((x_in, g_in, own_seq))
        x_seq = lax.all_to_all(x_in, "ctx", split_axis=1, concat_axis=0, tiled=True).reshape(rows * owners, width)
        g_seq = lax.all_to_all(g_in, "ctx", split_axis=1, concat_axis=0, tiled=True).reshape(rows * owners, width)
        raw_seq = lax.all_to_all(r3[:, :, sl], "ctx", split_axis=1, concat_axis=0, tiled=True).reshape(
            rows * owners, per_chunk
        )
        x_back, raw_back, gb, gc = chunk_backward(
            x_seq, g_seq, raw_seq, b_rows, c_rows, rate_own[sl], gain_own[sl]
        )
        x_parts.append(
            lax.all_to_all(x_back, "ctx", split_axis=0, concat_axis=1, tiled=True).reshape(rows, owners, 1, width)
        )
        raw_parts.append(
            lax.all_to_all(raw_back, "ctx", split_axis=0, concat_axis=1, tiled=True).reshape(rows, owners, 1, per_chunk)
        )
        grad_b_all = gb if grad_b_all is None else grad_b_all + gb
        grad_c_all = gc if grad_c_all is None else grad_c_all + gc
    grad_x = jnp.concatenate(x_parts, axis=2).reshape(rows, owners * per_owner * head_width)
    grad_dt = jnp.concatenate(raw_parts, axis=2).reshape(rows, heads_here)

    is_first = half == 0
    send = jnp.where(is_first, grad_c_all, grad_b_all)
    keep = jnp.where(is_first, grad_b_all, grad_c_all)
    mine = keep + lax.ppermute(send, "tp", [(0, 1), (1, 0)])
    parts = lax.all_to_all(mine.reshape(owners, rows, state), "ctx", split_axis=0, concat_axis=0, tiled=True)
    mine = parts.sum(axis=0)
    other = lax.ppermute(mine, "tp", [(0, 1), (1, 0)])
    grad_b = jnp.where(is_first, mine, other)
    grad_c = jnp.where(is_first, other, mine)
    return (grad_x, grad_b, grad_c, grad_dt)


def solution(mesh):
    in_specs = (
        P("ctx", "tp"),
        P("ctx", None),
        P("ctx", None),
        P("ctx", "tp"),
        P("tp"),
        P("tp"),
        P("ctx", "tp"),
    )
    out_specs = (P("ctx", "tp"), P("ctx", None), P("ctx", None), P("ctx", "tp"))
    return jax.shard_map(local, mesh=mesh, in_specs=in_specs, out_specs=out_specs, check_vma=False)
```

profile of v0, /device:TPU:12, one launch (start us, length us, event | category | flops | bytes accessed | tf_op | source)
XLA Modules:
  0.0 336.8 jit_solution(13651372698275420782)
XLA Ops:
  6.6 4.5 %collective-permute-done.1 = bf16[512,128]{1,0:T(8,128)(2,1)S(1)} collective-permute-done((bf16[512,128]{1,0:T(8,128)(2,1)S(1)}, bf16[512,128]{1,0:T(8,128)(2,1)S(1)}, u32[]{:S(2)}, u32[]{:S(2)}) %collective-permute-start.1) | collective-permute-done | bytes 131104 | tf_op jit(solution)/shard_map/ppermute | solution.py:90
  11.7 5.9 %collective-permute-done.2 = bf16[1024,128]{1,0:T(8,128)(2,1)S(1)} collective-permute-done((bf16[1024,128]{1,0:T(8,128)(2,1)S(1)}, bf16[1024,128]{1,0:T(8,128)(2,1)S(1)}, u32[]{:S(2)}, u32[]{:S(2)}) %collective-permute-start.2) | collective-permute-done | bytes 262176 | tf_op jit(solution)/shard_map/ppermute | solution.py:90
  21.0 5.1 %all-to-all-start.1 = ((bf16[256,16,4]{0,2,1:T(4,128)(2,1)}), bf16[256,16,4]{0,2,1:T(4,128)(2,1)S(1)}, u32[]{:S(2)}, u32[]{:S(2)}) async-start(bf16[256,16,4]{0,2,1:T(4,128)(2,1)} %reshape.129), calls=%async_computation.1 | async-start | bytes 65536 | tf_op jit(solution)/shard_map/all_to_all | solution.py:132
  28.6 3.3 copy.74
  31.9 7.8 %collective-permute-done.3 = bf16[2048,128]{1,0:T(8,128)(2,1)} collective-permute-done((bf16[2048,128]{1,0:T(8,128)(2,1)S(1)}, bf16[2048,128]{1,0:T(8,128)(2,1)}, u32[]{:S(2)}, u32[]{:S(2)}) %collective-permute-start.3) | collective-permute-done | bytes 524320 | tf_op jit(solution)/shard_map/ppermute | solution.py:90
  41.5 55.7 %all_to_all.79 = bf16[256,16,256]{0,2,1:T(8,128)(2,1)} all-to-all(bf16[256,16,256]{0,2,1:T(8,128)(2,1)S(1)} %bitcast.188), channel_id=1, replica_groups=mesh['ctx'=16,'tp'=2] {'ctx'}, dimensions={1} | all-to-all | bytes 4194304 | tf_op jit(solution)/shard_map/all_to_all | solution.py:131
  97.2 6.3 %all-to-all-start.3 = ((bf16[256,16,256]{0,2,1:T(8,128)(2,1)}), bf16[256,16,256]{0,2,1:T(8,128)(2,1)}, u32[]{:S(2)}, u32[]{:S(2)}) async-start(bf16[256,16,256]{0,2,1:T(8,128)(2,1)} %bitcast), calls=%async_computation.3 | async-start | bytes 4194304 | tf_op jit(solution)/shard_map/all_to_all | solution.py:130
  114.5 36.3 %all-to-all-done.3 = bf16[256,16,256]{0,2,1:T(8,128)(2,1)} async-done(((bf16[256,16,256]{0,2,1:T(8,128)(2,1)}), bf16[256,16,256]{0,2,1:T(8,128)(2,1)}, u32[]{:S(2)}, u32[]{:S(2)}) %all-to-all-start.3) | async-done | bytes 2097184 | tf_op jit(solution)/shard_map/all_to_all | solution.py:130
  150.7 4.1 %copy.87 = bf16[16,256,1,256]{1,0,3,2:T(8,128)(2,1)} copy(bf16[16,256,1,256]{1,3,0,2:T(8,128)(2,1)} %bitcast.25) | data formatting | bytes 4194304 | tf_op jit(solution)/shard_map/all_to_all | solution.py:130
  157.7 5.9 %multiply_reduce_fusion.4 = (f32[4,16]{1,0:T(4,128)}, f32[4,16,64,128]{3,2,1,0:T(8,128)S(1)}) fusion(f32[16,256,128]{1,2,0:T(8,128)} %copy.77, f32[4,16,256]{2,1,0:T(8,128)S(1)} %get-tuple-element.38, bf16[4,8,16,8,256]{4,3,2,1,0:T(8,128)(2,1)} %bitcast.177), kind=kOutput, calls=%fused_computation.40 | convolution fusion | flops 808452032 | bytes 6357248 | tf_op jit(solution)/shard_map/transpose(jvp(vmap(kin,kpn->kip)))/dot_general | solution.py:51
  165.6 3.9 %fusion.10 = (f32[4,16,256]{2,0,1:T(4,128)S(1)}, f32[16,4,64,256]{3,2,1,0:T(8,128)}) fusion(bf16[4,8,16,8,256]{4,3,2,1,0:T(8,128)(2,1)S(1)} %bitcast.169, bf16[16,256,128,1]{2,1,3,0:T(8,128)(2,1)S(1)} %bitcast.174, f32[16,4,64,128]{3,0,2,1:T(8,128)S(1)} %fusion.44), kind=kOutput, calls=%fused_computation.18 | convolution fusion | flops 808435712 | bytes 9502720 | tf_op jit(solution)/shard_map/transpose(jvp(vmap(kjp,kjn->kpn)))/dot_general | solution.py:38
  169.6 16.2 %fusion.5 = (f32[4,16,256]{2,1,0:T(8,128)}, f32[4,16,256]{2,1,0:T(8,128)}, f32[4,16,256]{2,1,0:T(8,128)S(1)}, f32[16,256,256]{2,1,0:T(8,128)}, f32[4,16,256,256]{3,2,1,0:T(8,128)}) fusion(f32[4,16,256]{2,1,0:T(8,128)S(1)} %bitcast.200, f32[4,16,256]{2,1,0:T(8,128)S(1)} %get-tuple-element.39, f32[16,256,256]{2,1,0:T(8,128)S(1)} %copy-done.11, ...), kind=kOutput, calls=%fused_computation.9 | convolution fusion | flops 594493440 | bytes 29753344 | tf_op jit(solution)/shard_map/transpose(jvp(vmap(kij,kjp->kip)))/dot_general | solution.py:35
  187.9 5.2 %fusion.9 = f32[16,256,128,1]{2,1,3,0:T(8,128)} fusion(f32[4,16,256]{2,0,1:T(4,128)S(1)} %copy.76, f32[16,4,64,128]{3,0,2,1:T(8,128)S(1)} %fusion.44, bf16[4,8,16,8,256]{4,3,2,1,0:T(8,128)(2,1)S(1)} %bitcast.172), kind=kOutput, calls=%fused_computation.17 | convolution fusion | flops 807403520 | bytes 6356992 | tf_op jit(solution)/shard_map/transpose(jvp(vmap(kjp,kjn->kpn)))/dot_general | solution.py:38
  195.2 5.1 %multiply_reduce_fusion.2 = (f32[4,16,256]{2,1,0:T(8,128)}, f32[16,256,128]{1,2,0:T(8,128)}) fusion(f32[16,256,128]{1,2,0:T(8,128)S(1)} %copy-done.12, f32[4,16,256]{2,1,0:T(8,128)S(1)} %copy-done.16, f32[4,16,64,128]{3,1,2,0:T(8,128)S(1)} %fusion.47, bf16[4,8,16,8,256]{4,3,2,1,0:T(8,128)(2,1)S(1)} %bitcast.179), kind=kOutput, calls=%fused_computation.10 | convolution fusion | flops 813154304 | bytes 8519680 | tf_op jit(solution)/shard_map/transpose(jvp(vmap(kin,kpn->kip)))/dot_general | solution.py:51
  202.5 3.7 %convolution_add_fusion = f32[16,256,128]{2,1,0:T(8,128)S(1)} fusion(f32[16,256,128]{2,1,0:T(8,128)S(1)} %copy.96, f32[16,256,256]{2,1,0:T(8,128)} %get-tuple-element.19, bf16[16,256,128]{2,1,0:T(8,128)(2,1)S(1)} %bitcast.176), kind=kOutput, calls=%fused_computation.55 | convolution fusion | flops 805830656 | bytes 9437184 | tf_op jit(solution)/shard_map/transpose(jvp(vmap(kin,kjn->kij)))/dot_general | solution.py:31
  206.9 3.8 %broadcast_select_fusion.1 = (f32[16,256,128]{2,1,0:T(8,128)S(1)}, f32[16,256,128]{2,1,0:T(8,128)}) fusion(f32[16,256,128]{2,1,0:T(8,128)S(1)} %convolution_add_fusion, pred[]{:T(512)S(6)} %eq.35, f32[16,256,256]{2,1,0:T(8,128)S(1)} %copy-done.4, bf16[16,256,128]{2,1,0:T(8,128)(2,1)S(1)} %bitcast.184, f32[16,256,128,1]{2,1,3,0:T(8,128)S(1)} %copy-done.10), kind=kOutput, calls=%fused_computation.70 | convolution fusion | flops 806879232 | bytes 13631489 | tf_op jit(solution)/shard_map/transpose(jvp(vmap(kin,kjn->kij)))/dot_general | solution.py:31
  210.8 3.7 %fusion.111 = (f32[4,16]{1,0:T(4,128)S(1)}, f32[4,16]{1,0:T(4,128)S(1)}) fusion(f32[4,16]{1,0:T(4,128)S(1)} %get-tuple-element.40, f32[4,16]{1,0:T(4,128)S(1)} %get-tuple-element.25, f32[16,4,64,128]{3,2,1,0:T(8,128)S(1)} %copy-done.1, f32[4,16,64,128]{3,2,1,0:T(8,128)S(1)} %copy-done.8, pred[16,16]{1,0:T(8,128)(4,1)S(1)} %iota_compare_fusion.6), kind=kOutput, calls=%fused_computation.134 | convolution fusion | flops 50337664 | bytes 4195584 | tf_op jit(solution)/shard_map/transpose(jvp(vmap(kj,jpn->kpn)))/dot_general | solution.py:47
  215.9 4.7 %all-to-all-start.5 = ((bf16[16,256,4]{1,2,0:T(4,128)(2,1)}), bf16[16,256,4]{1,2,0:T(4,128)(2,1)S(1)}, u32[]{:S(2)}, u32[]{:S(2)}) async-start(bf16[16,256,4]{1,2,0:T(4,128)(2,1)} %bitcast.40), calls=%async_computation.5 | async-start | bytes 65536 | tf_op jit(solution)/shard_map/all_to_all | solution.py:142
  220.5 3.1 bitcast_add_fusion.1
  225.8 7.0 %all-to-all-start.4 = ((f32[16,256,128]{2,1,0:T(8,128)}), f32[16,256,128]{2,1,0:T(8,128)}, u32[]{:S(2)}, u32[]{:S(2)}) async-start(f32[16,256,128]{2,1,0:T(8,128)} %bitcast.185), calls=%async_computation.4 | async-start | bytes 4194304 | tf_op jit(solution)/shard_map/all_to_all | solution.py:153
  232.9 9.0 %fusion.12 = f32[16,4,8,8,256]{4,3,2,1,0:T(8,128)S(1)} fusion(f32[16,4,64,256]{3,2,1,0:T(8,128)} %get-tuple-element.42, f32[4,16,256]{2,0,1:T(4,128)S(1)} %copy.76, bf16[4,8,16,8,256]{4,3,2,1,0:T(8,128)(2,1)S(1)} %bitcast.180, f32[4,16,256,256]{3,2,1,0:T(8,128)} %get-tuple-element.26), kind=kOutput, calls=%fused_computation.21 | convolution fusion | flops 1612709888 | bytes 27328512 | tf_op jit(solution)/shard_map/transpose(jvp(vmap(kij,kjp->kip)))/dot_general | solution.py:35
  245.9 34.7 %all-to-all-done.4 = f32[16,256,128]{2,1,0:T(8,128)} async-done(((f32[16,256,128]{2,1,0:T(8,128)}), f32[16,256,128]{2,1,0:T(8,128)}, u32[]{:S(2)}, u32[]{:S(2)}) %all-to-all-start.4) | async-done | bytes 2097184 | tf_op jit(solution)/shard_map/all_to_all | solution.py:153
  280.6 4.7 %all-to-all-start.2 = ((bf16[16,256,256]{1,2,0:T(8,128)(2,1)}), bf16[16,256,256]{1,2,0:T(8,128)(2,1)S(1)}, u32[]{:S(2)}, u32[]{:S(2)}) async-start(bf16[16,256,256]{1,2,0:T(8,128)(2,1)} %copy.86), calls=%async_computation.2 | async-start | bytes 4194304 | tf_op jit(solution)/shard_map/all_to_all | solution.py:139
  287.7 45.2 %all-to-all-done.2 = bf16[16,256,256]{1,2,0:T(8,128)(2,1)S(1)} async-done(((bf16[16,256,256]{1,2,0:T(8,128)(2,1)}), bf16[16,256,256]{1,2,0:T(8,128)(2,1)S(1)}, u32[]{:S(2)}, u32[]{:S(2)}) %all-to-all-start.2) | async-done | bytes 2097184 | tf_op jit(solution)/shard_map/all_to_all | solution.py:139
  (114 shorter events, 50.6 us)
Async XLA Ops:
  0.6 19.8 %copy-start.21 = (bf16[256,64]{0,1:T(8,128)(2,1)S(1)}, bf16[256,64]{0,1:T(8,128)(2,1)}, u32[]{:S(2)}) copy-start(bf16[256,64]{0,1:T(8,128)(2,1)} %param.10) | copy-start | bytes 98308
  0.6 25.5 %copy-start.14 = (bf16[256,4096]{1,0:T(8,128)(2,1)S(1)}, bf16[256,4096]{1,0:T(8,128)(2,1)}, u32[]{:S(2)}) copy-start(bf16[256,4096]{1,0:T(8,128)(2,1)} %param.7) | copy-start | bytes 6291460
  1.7 4.3 %collective-permute-start = (bf16[256,128]{1,0:T(8,128)(2,1)S(1)}, bf16[256,128]{1,0:T(8,128)(2,1)S(1)}, u32[]{:S(2)}, u32[]{:S(2)}) collective-permute-start(bf16[256,128]{1,0:T(8,128)(2,1)S(1)} %broadcast_select_fusion.6), channel_id=1, source_target_pairs={{0,2},{2,0},{4,6},{6,4},{8,10},{10,8},{12,14},{14,12},{16,18},{18,... | collective-permute-start | bytes 196616 | tf_op jit(solution)/shard_map/ppermute | solution.py:90
  6.0 5.0 %collective-permute-start.1 = (bf16[512,128]{1,0:T(8,128)(2,1)S(1)}, bf16[512,128]{1,0:T(8,128)(2,1)S(1)}, u32[]{:S(2)}, u32[]{:S(2)}) collective-permute-start(bf16[512,128]{1,0:T(8,128)(2,1)S(1)} %maximum_select_fusion.3), channel_id=1, source_target_pairs={{0,4},{2,6},{4,0},{6,2},{8,12},{10,14},{12,8},{14,10},{16,20},{18,... | collective-permute-start | bytes 393224 | tf_op jit(solution)/shard_map/ppermute | solution.py:90
  11.2 6.4 %collective-permute-start.2 = (bf16[1024,128]{1,0:T(8,128)(2,1)S(1)}, bf16[1024,128]{1,0:T(8,128)(2,1)S(1)}, u32[]{:S(2)}, u32[]{:S(2)}) collective-permute-start(bf16[1024,128]{1,0:T(8,128)(2,1)S(1)} %maximum_select_fusion.2), channel_id=1, source_target_pairs={{0,8},{2,10},{4,12},{6,14},{8,0},{10,2},{12,4},{14,6},{16,24},{18,... | collective-permute-start | bytes 786440 | tf_op jit(solution)/shard_map/ppermute | solution.py:90
  17.7 10.9 %copy-start.13 = (bf16[2048,128]{1,0:T(8,128)(2,1)}, bf16[2048,128]{1,0:T(8,128)(2,1)S(1)}, u32[]{:S(2)}) copy-start(bf16[2048,128]{1,0:T(8,128)(2,1)S(1)} %maximum_select_fusion.1) | copy-start | bytes 1572868
  17.7 22.0 %collective-permute-start.3 = (bf16[2048,128]{1,0:T(8,128)(2,1)S(1)}, bf16[2048,128]{1,0:T(8,128)(2,1)}, u32[]{:S(2)}, u32[]{:S(2)}) collective-permute-start(bf16[2048,128]{1,0:T(8,128)(2,1)S(1)} %maximum_select_fusion.1), channel_id=1, source_target_pairs={{0,16},{2,18},{4,20},{6,22},{8,24},{10,26},{12,28},{14,30},{16,0},... | collective-permute-start | bytes 1572872 | tf_op jit(solution)/shard_map/ppermute | solution.py:90
  21.0 20.5 %all-to-all-start.1 = ((bf16[256,16,4]{0,2,1:T(4,128)(2,1)}), bf16[256,16,4]{0,2,1:T(4,128)(2,1)S(1)}, u32[]{:S(2)}, u32[]{:S(2)}) async-start(bf16[256,16,4]{0,2,1:T(4,128)(2,1)} %reshape.129), calls=%async_computation.1 | async-start | bytes 65536 | tf_op jit(solution)/shard_map/all_to_all | solution.py:132
  97.2 6.3 %copy-start.26 = (f32[64]{0:T(128)S(1)}, f32[64]{0:T(128)}, u32[]{:S(2)}) copy-start(f32[64]{0:T(128)} %param.11) | copy-start | bytes 772
  97.2 53.5 %all-to-all-start.3 = ((bf16[256,16,256]{0,2,1:T(8,128)(2,1)}), bf16[256,16,256]{0,2,1:T(8,128)(2,1)}, u32[]{:S(2)}, u32[]{:S(2)}) async-start(bf16[256,16,256]{0,2,1:T(8,128)(2,1)} %bitcast), calls=%async_computation.3 | async-start | bytes 4194304 | tf_op jit(solution)/shard_map/all_to_all | solution.py:130
  103.6 2.7 collective-permute-start.4
  104.7 53.0 %copy-start.15 = (f32[4,16,256]{2,1,0:T(8,128)}, f32[4,16,256]{2,1,0:T(8,128)S(1)}, u32[]{:S(2)}) copy-start(f32[4,16,256]{2,1,0:T(8,128)S(1)} %get-tuple-element.38) | copy-start | bytes 196612
  106.5 4.4 %copy-start.5 = (bf16[4096,128]{1,0:T(8,128)(2,1)}, bf16[4096,128]{1,0:T(8,128)(2,1)S(1)}, u32[]{:S(2)}) copy-start(bf16[4096,128]{1,0:T(8,128)(2,1)S(1)} %get-tuple-element.29) | copy-start | bytes 3145732
  187.9 5.3 %copy-start = (f32[16,4,64,128]{3,2,1,0:T(8,128)}, f32[16,4,64,128]{3,2,1,0:T(8,128)S(1)}, u32[]{:S(2)}) copy-start(f32[16,4,64,128]{3,2,1,0:T(8,128)S(1)} %fusion.8) | copy-start | bytes 6291460
  187.9 5.2 %copy-start.22 = (f32[4,16]{1,0:T(4,128)S(1)}, f32[4,16]{1,0:T(4,128)}, u32[]{:S(2)}) copy-start(f32[4,16]{1,0:T(4,128)} %get-tuple-element.24) | copy-start | bytes 772
  202.5 4.4 %copy-start.10 = (f32[16,256,128,1]{2,1,3,0:T(8,128)S(1)}, f32[16,256,128,1]{2,1,3,0:T(8,128)}, u32[]{:S(2)}) copy-start(f32[16,256,128,1]{2,1,3,0:T(8,128)} %fusion.9) | copy-start | bytes 6291460
  210.7 4.4 %copy-start.25 = (f32[4]{0:T(128)S(1)}, f32[4]{0:T(128)}, u32[]{:S(2)}) copy-start(f32[4]{0:T(128)} %copy-done.24) | copy-start | bytes 52
  210.7 9.8 %collective-permute-start.5 = (f32[4096,128]{1,0:T(8,128)}, f32[4096,128]{1,0:T(8,128)}, u32[]{:S(2)}, u32[]{:S(2)}) collective-permute-start(f32[4096,128]{1,0:T(8,128)} %bitcast.34), channel_id=1, source_target_pairs={{0,1},{1,0},{2,3},{3,2},{4,5},{5,4},{6,7},{7,6},{8,9},{9,8},{10,11... | collective-permute-start | bytes 6291464 | tf_op jit(solution)/shard_map/ppermute | solution.py:152
  215.9 9.9 %all-to-all-start.5 = ((bf16[16,256,4]{1,2,0:T(4,128)(2,1)}), bf16[16,256,4]{1,2,0:T(4,128)(2,1)S(1)}, u32[]{:S(2)}, u32[]{:S(2)}) async-start(bf16[16,256,4]{1,2,0:T(4,128)(2,1)} %bitcast.40), calls=%async_computation.5 | async-start | bytes 65536 | tf_op jit(solution)/shard_map/all_to_all | solution.py:142
  225.8 7.0 %copy-start.27 = (f32[64]{0:T(128)S(1)}, f32[64]{0:T(128)}, u32[]{:S(2)}) copy-start(f32[64]{0:T(128)} %param.12) | copy-start | bytes 772
  225.8 7.1 %copy-start.3 = (bf16[4096,4,64]{0,2,1:T(8,128)(2,1)S(1)}, bf16[4096,4,64]{0,2,1:T(8,128)(2,1)}, u32[]{:S(2)}) copy-start(bf16[4096,4,64]{0,2,1:T(8,128)(2,1)} %reshape.128) | copy-start | bytes 6291460
  225.8 54.9 %all-to-all-start.4 = ((f32[16,256,128]{2,1,0:T(8,128)}), f32[16,256,128]{2,1,0:T(8,128)}, u32[]{:S(2)}, u32[]{:S(2)}) async-start(f32[16,256,128]{2,1,0:T(8,128)} %bitcast.185), calls=%async_computation.4 | async-start | bytes 4194304 | tf_op jit(solution)/shard_map/all_to_all | solution.py:153
  280.6 52.4 %all-to-all-start.2 = ((bf16[16,256,256]{1,2,0:T(8,128)(2,1)}), bf16[16,256,256]{1,2,0:T(8,128)(2,1)S(1)}, u32[]{:S(2)}, u32[]{:S(2)}) async-start(bf16[16,256,256]{1,2,0:T(8,128)(2,1)} %copy.86), calls=%async_computation.2 | async-start | bytes 4194304 | tf_op jit(solution)/shard_map/all_to_all | solution.py:139
  287.0 48.8 %collective-permute-start.6 = (f32[256,128]{1,0:T(8,128)S(1)}, f32[256,128]{1,0:T(8,128)S(1)}, u32[]{:S(2)}, u32[]{:S(2)}) collective-permute-start(f32[256,128]{1,0:T(8,128)S(1)} %reduce_sum.107), channel_id=1, source_target_pairs={{0,1},{1,0},{2,3},{3,2},{4,5},{5,4},{6,7},{7,6},{8,9},{9,8},{10,11... | collective-permute-start | bytes 393224 | tf_op jit(solution)/shard_map/ppermute | solution.py:155
  (17 other events, 56.5 us)
where the time goes:
time: 340 us; the launch traced here: 337 us
  waiting for transfers between devices  140 us (41%)
  matrix products  65.7 us (19%)
  blocking collectives  55.7 us (16%)
  starting transfers between devices  33.3 us (10%)
  local copies, waits for them, and re-layouts  29.4 us (9%)
  other arithmetic  11.2 us (3%)
    all_to_all x1, blocking collectives, local(): lax.all_to_all(g_in, 'ctx', split_axis=1, concat_axis=0, tiled=True)  55.7 us
    all_to_all x1, waiting for transfers between devices, local(): lax.all_to_all(x_back, 'ctx', split_axis=0, concat_axis=1, tiled=True)  45.2 us
    all_to_all x1, waiting for transfers between devices, local(): lax.all_to_all(x_in, 'ctx', split_axis=1, concat_axis=0, tiled=True)  36.3 us
    all_to_all x1, waiting for transfers between devices, local(): lax.all_to_all(mine.reshape(owners, rows, state), 'ctx', split_axis=0, co...  34.7 us
    dot_general x2, matrix products, head_forward(): output = jnp.einsum('kij,kjp->kip', scores, x_blocks, precision=precise)  25.2 us
    ppermute x4, waiting for transfers between devices, gather_ctx(): theirs = lax.ppermute(have, 'ctx', [(k, k ^ step) for k in range(owners)])  20.9 us
    dot_general x2, matrix products, head_forward(): jnp.einsum('kin,kpn->kip', reading, entering, precision=precise)  11 us
    unnamed x65, local copies, waits for them, and re-layouts  10.8 us
  transfers between devices with their start and end apart: 12, of which 9 were waited for; matrix products, arithmetic and copies ran while one was open for 13% of the time, Pallas kernels for 0%

commit v1 on v0

--- a/solution.py
+++ b/solution.py
@@ -126,7 +126,7 @@
         x_in = x4[:, :, sl, :].reshape(rows, owners, width)
         g_in = g4[:, :, sl, :].reshape(rows, owners, width)
         if c == 0:
-            x_in, g_in, _ = lax.optimization_barrier((x_in, g_in, own_seq))
+            g_in, _ = lax.optimization_barrier((g_in, own_seq))
         x_seq = lax.all_to_all(x_in, "ctx", split_axis=1, concat_axis=0, tiled=True).reshape(rows * owners, width)
         g_seq = lax.all_to_all(g_in, "ctx", split_axis=1, concat_axis=0, tiled=True).reshape(rows * owners, width)
         raw_seq = lax.all_to_all(r3[:, :, sl], "ctx", split_axis=1, concat_axis=0, tiled=True).reshape(

time: 340 us -> 336 us (0.988)
  blocking collectives: 55.7 us -> 0 us
  waiting for transfers between devices: 140 us -> 173 us
  starting transfers between devices: 33.3 us -> 47.1 us
  local copies, waits for them, and re-layouts: 29.4 us -> 35.7 us
    all_to_all x1 -> x0, blocking collectives: 55.7 us -> none  [local(): lax.all_to_all(g_in, 'ctx', split_axis=1, concat_axis=0, tiled=True)]
    all_to_all x1, waiting for transfers between devices: 36.3 us -> 0.01 us  [local(): lax.all_to_all(x_in, 'ctx', split_axis=1, concat_axis=0, tiled=True)]
    ppermute x4, waiting for transfers between devices: 20.9 us -> 54.9 us  [gather_ctx(): theirs = lax.ppermute(have, 'ctx', [(k, k ^ step) for k in range(owners)])]
    all_to_all x0 -> x1, waiting for transfers between devices: none -> 33.7 us  [local(): lax.all_to_all(g_in, 'ctx', split_axis=1, concat_axis=0, tiled=True)]
    all_to_all x0 -> x1, starting transfers between devices: none -> 8.33 us  [local(): lax.all_to_all(g_in, 'ctx', split_axis=1, concat_axis=0, tiled=True)]
    unnamed x65 -> x67, local copies, waits for them, and re-layouts: 10.8 us -> 13.2 us
  transfers between devices with their start and end apart: 12 -> 13, of which waited for: 9 -> 10; matrix products, arithmetic and copies ran while one was open for 13% -> 14% of each run, Pallas kernels for 0% -> 0%
where the time goes in v1:
time: 336 us; the launch traced here: 333 us
  waiting for transfers between devices  173 us (51%)
  matrix products  65.7 us (20%)
  starting transfers between devices  47.1 us (14%)
  local copies, waits for them, and re-layouts  35.7 us (11%)
  other arithmetic  10.2 us (3%)
    ppermute x4, waiting for transfers between devices, gather_ctx(): theirs = lax.ppermute(have, 'ctx', [(k, k ^ step) for k in range(owners)])  54.9 us
    all_to_all x1, waiting for transfers between devices, local(): lax.all_to_all(x_back, 'ctx', split_axis=0, concat_axis=1, tiled=True)  45.2 us
    all_to_all x1, waiting for transfers between devices, local(): lax.all_to_all(mine.reshape(owners, rows, state), 'ctx', split_axis=0, co...  34.7 us
    all_to_all x1, waiting for transfers between devices, local(): lax.all_to_all(g_in, 'ctx', split_axis=1, concat_axis=0, tiled=True)  33.7 us
    dot_general x2, matrix products, head_forward(): output = jnp.einsum('kij,kjp->kip', scores, x_blocks, precision=precise)  25.2 us
    unnamed x67, local copies, waits for them, and re-layouts  13.2 us
    dot_general x2, matrix products, head_forward(): jnp.einsum('kin,kpn->kip', reading, entering, precision=precise)  11 us
    dot_general x3, matrix products, head_forward(): states = jnp.einsum('kjp,kjn->kpn', weighted, b_blocks, precision=precise)  10.4 us
  transfers between devices with their start and end apart: 13, of which 10 were waited for; matrix products, arithmetic and copies ran while one was open for 14% of the time, Pallas kernels for 0%

profile of v1, /device:TPU:12, one launch (start us, length us, event | category | flops | bytes accessed | tf_op | source)
XLA Modules:
  0.0 332.9 jit_solution(14775902268051593964)
XLA Ops:
  2.0 7.2 %all-to-all-start.1 = ((bf16[256,16,4]{0,2,1:T(4,128)(2,1)}), bf16[256,16,4]{0,2,1:T(4,128)(2,1)S(1)}, u32[]{:S(2)}, u32[]{:S(2)}) async-start(bf16[256,16,4]{0,2,1:T(4,128)(2,1)} %reshape.129), calls=%async_computation.1 | async-start | bytes 65536 | tf_op jit(solution)/shard_map/all_to_all | solution.py:132
  9.2 4.1 %copy.86 = bf16[256,4096]{0,1:T(8,128)(2,1)} copy(bf16[256,4096]{1,0:T(8,128)(2,1)} %param.7) | data formatting | bytes 4194304 | tf_op args[0]
  14.4 5.9 %all-to-all-start.3 = ((bf16[256,16,256]{0,2,1:T(8,128)(2,1)}), bf16[256,16,256]{0,2,1:T(8,128)(2,1)S(1)}, u32[]{:S(2)}, u32[]{:S(2)}) async-start(bf16[256,16,256]{0,2,1:T(8,128)(2,1)} %bitcast.187), calls=%async_computation.3 | async-start | bytes 4194304 | tf_op jit(solution)/shard_map/all_to_all | solution.py:130
  21.9 6.7 %collective-permute-done = bf16[256,128]{1,0:T(8,128)(2,1)S(1)} collective-permute-done((bf16[256,128]{1,0:T(8,128)(2,1)S(1)}, bf16[256,128]{1,0:T(8,128)(2,1)S(1)}, u32[]{:S(2)}, u32[]{:S(2)}) %collective-permute-start) | collective-permute-done | bytes 65568 | tf_op jit(solution)/shard_map/ppermute | solution.py:90
  29.5 4.9 %collective-permute-done.1 = bf16[512,128]{1,0:T(8,128)(2,1)S(1)} collective-permute-done((bf16[512,128]{1,0:T(8,128)(2,1)S(1)}, bf16[512,128]{1,0:T(8,128)(2,1)S(1)}, u32[]{:S(2)}, u32[]{:S(2)}) %collective-permute-start.1) | collective-permute-done | bytes 131104 | tf_op jit(solution)/shard_map/ppermute | solution.py:90
  37.2 22.8 %collective-permute-done.2 = bf16[1024,128]{1,0:T(8,128)(2,1)S(1)} collective-permute-done((bf16[1024,128]{1,0:T(8,128)(2,1)S(1)}, bf16[1024,128]{1,0:T(8,128)(2,1)S(1)}, u32[]{:S(2)}, u32[]{:S(2)}) %collective-permute-start.2) | collective-permute-done | bytes 262176 | tf_op jit(solution)/shard_map/ppermute | solution.py:90
  63.7 4.1 %copy.73 = bf16[256,4096]{0,1:T(8,128)(2,1)} copy(bf16[256,4096]{1,0:T(8,128)(2,1)} %param.13) | data formatting | bytes 4194304 | tf_op args[6]
  67.8 20.4 %collective-permute-done.3 = bf16[2048,128]{1,0:T(8,128)(2,1)} collective-permute-done((bf16[2048,128]{1,0:T(8,128)(2,1)S(1)}, bf16[2048,128]{1,0:T(8,128)(2,1)}, u32[]{:S(2)}, u32[]{:S(2)}) %collective-permute-start.3) | collective-permute-done | bytes 524320 | tf_op jit(solution)/shard_map/ppermute | solution.py:90
  90.1 8.3 %all-to-all-start = ((bf16[256,16,256]{0,2,1:T(8,128)(2,1)}), bf16[256,16,256]{0,2,1:T(8,128)(2,1)}, u32[]{:S(2)}, u32[]{:S(2)}) async-start(bf16[256,16,256]{0,2,1:T(8,128)(2,1)} %bitcast.188), calls=%async_computation | async-start | bytes 4194304 | tf_op jit(solution)/shard_map/all_to_all | solution.py:131
  111.2 33.7 %all-to-all-done = bf16[256,16,256]{0,2,1:T(8,128)(2,1)} async-done(((bf16[256,16,256]{0,2,1:T(8,128)(2,1)}), bf16[256,16,256]{0,2,1:T(8,128)(2,1)}, u32[]{:S(2)}, u32[]{:S(2)}) %all-to-all-start) | async-done | bytes 2097184 | tf_op jit(solution)/shard_map/all_to_all | solution.py:131
  144.9 4.1 %copy.74 = bf16[16,256,1,256]{1,0,3,2:T(8,128)(2,1)} copy(bf16[16,256,1,256]{1,3,0,2:T(8,128)(2,1)} %bitcast.2) | data formatting | bytes 4194304 | tf_op jit(solution)/shard_map/all_to_all | solution.py:131
  149.0 4.3 %reshape.128 = bf16[4096,4,64]{0,2,1:T(8,128)(2,1)} reshape(bf16[16,256,1,256]{1,0,3,2:T(8,128)(2,1)} %copy.74) | data formatting | bytes 4194304 | tf_op jit(solution)/shard_map/reshape | solution.py:131
  153.3 5.9 %multiply_reduce_fusion.4 = (f32[4,16]{1,0:T(4,128)}, f32[4,16,64,128]{3,2,1,0:T(8,128)S(1)}) fusion(f32[16,256,128]{1,2,0:T(8,128)} %copy.76, f32[4,16,256]{2,1,0:T(8,128)S(1)} %get-tuple-element.36, bf16[4,8,16,8,256]{4,3,2,1,0:T(8,128)(2,1)} %bitcast.177), kind=kOutput, calls=%fused_computation.40 | convolution fusion | flops 808452032 | bytes 6357248 | tf_op jit(solution)/shard_map/transpose(jvp(vmap(kin,kpn->kip)))/dot_general | solution.py:51
  161.2 3.9 %fusion.10 = (f32[4,16,256]{2,0,1:T(4,128)S(1)}, f32[16,4,64,256]{3,2,1,0:T(8,128)}) fusion(bf16[4,8,16,8,256]{4,3,2,1,0:T(8,128)(2,1)S(1)} %bitcast.169, bf16[16,256,128,1]{2,1,3,0:T(8,128)(2,1)S(1)} %bitcast.174, f32[16,4,64,128]{3,0,2,1:T(8,128)S(1)} %fusion.44), kind=kOutput, calls=%fused_computation.18 | convolution fusion | flops 808435712 | bytes 9502720 | tf_op jit(solution)/shard_map/transpose(jvp(vmap(kjp,kjn->kpn)))/dot_general | solution.py:38
  165.1 16.3 %fusion.5 = (f32[4,16,256]{2,1,0:T(8,128)}, f32[4,16,256]{2,1,0:T(8,128)}, f32[4,16,256]{2,1,0:T(8,128)S(1)}, f32[16,256,256]{2,1,0:T(8,128)}, f32[4,16,256,256]{3,2,1,0:T(8,128)}) fusion(f32[4,16,256]{2,1,0:T(8,128)S(1)} %bitcast.201, f32[4,16,256]{2,1,0:T(8,128)S(1)} %get-tuple-element.37, f32[16,256,256]{2,1,0:T(8,128)S(1)} %copy-done.12, ...), kind=kOutput, calls=%fused_computation.9 | convolution fusion | flops 594493440 | bytes 29753344 | tf_op jit(solution)/shard_map/transpose(jvp(vmap(kij,kjp->kip)))/dot_general | solution.py:35
  183.5 5.2 %fusion.9 = f32[16,256,128,1]{2,1,3,0:T(8,128)} fusion(f32[4,16,256]{2,0,1:T(4,128)S(1)} %copy.75, f32[16,4,64,128]{3,0,2,1:T(8,128)S(1)} %fusion.44, bf16[4,8,16,8,256]{4,3,2,1,0:T(8,128)(2,1)S(1)} %bitcast.172), kind=kOutput, calls=%fused_computation.17 | convolution fusion | flops 807403520 | bytes 6356992 | tf_op jit(solution)/shard_map/transpose(jvp(vmap(kjp,kjn->kpn)))/dot_general | solution.py:38
  190.8 5.1 %multiply_reduce_fusion.2 = (f32[4,16,256]{2,1,0:T(8,128)}, f32[16,256,128]{1,2,0:T(8,128)}) fusion(f32[16,256,128]{1,2,0:T(8,128)S(1)} %copy-done.13, f32[4,16,256]{2,1,0:T(8,128)S(1)} %copy-done.18, f32[4,16,64,128]{3,1,2,0:T(8,128)S(1)} %fusion.47, bf16[4,8,16,8,256]{4,3,2,1,0:T(8,128)(2,1)S(1)} %bitcast.179), kind=kOutput, calls=%fused_computation.10 | convolution fusion | flops 813154304 | bytes 8519680 | tf_op jit(solution)/shard_map/transpose(jvp(vmap(kin,kpn->kip)))/dot_general | solution.py:51
  202.5 3.8 %broadcast_select_fusion.1 = (f32[16,256,128]{2,1,0:T(8,128)S(1)}, f32[16,256,128]{2,1,0:T(8,128)}) fusion(f32[16,256,128]{2,1,0:T(8,128)S(1)} %convolution_add_fusion, pred[]{:T(512)S(6)} %eq.35, f32[16,256,256]{2,1,0:T(8,128)S(1)} %copy-done.4, bf16[16,256,128]{2,1,0:T(8,128)(2,1)S(1)} %bitcast.184, f32[16,256,128,1]{2,1,3,0:T(8,128)S(1)} %copy-done.11), kind=kOutput, calls=%fused_computation.70 | convolution fusion | flops 806879232 | bytes 13631489 | tf_op jit(solution)/shard_map/transpose(jvp(vmap(kin,kjn->kij)))/dot_general | solution.py:31
  211.4 5.2 %all-to-all-start.5 = ((bf16[16,256,4]{1,2,0:T(4,128)(2,1)}), bf16[16,256,4]{1,2,0:T(4,128)(2,1)S(1)}, u32[]{:S(2)}, u32[]{:S(2)}) async-start(bf16[16,256,4]{1,2,0:T(4,128)(2,1)} %bitcast.40), calls=%async_computation.5 | async-start | bytes 65536 | tf_op jit(solution)/shard_map/all_to_all | solution.py:142
  221.9 7.0 %all-to-all-start.4 = ((f32[16,256,128]{2,1,0:T(8,128)}), f32[16,256,128]{2,1,0:T(8,128)}, u32[]{:S(2)}, u32[]{:S(2)}) async-start(f32[16,256,128]{2,1,0:T(8,128)} %bitcast.185), calls=%async_computation.4 | async-start | bytes 4194304 | tf_op jit(solution)/shard_map/all_to_all | solution.py:153
  229.0 9.0 %fusion.12 = f32[16,4,8,8,256]{4,3,2,1,0:T(8,128)S(1)} fusion(f32[16,4,64,256]{3,2,1,0:T(8,128)} %get-tuple-element.40, f32[4,16,256]{2,0,1:T(4,128)S(1)} %copy.75, bf16[4,8,16,8,256]{4,3,2,1,0:T(8,128)(2,1)S(1)} %bitcast.180, f32[4,16,256,256]{3,2,1,0:T(8,128)} %get-tuple-element.24), kind=kOutput, calls=%fused_computation.21 | convolution fusion | flops 1612709888 | bytes 27328512 | tf_op jit(solution)/shard_map/transpose(jvp(vmap(kij,kjp->kip)))/dot_general | solution.py:35
  242.0 34.7 %all-to-all-done.4 = f32[16,256,128]{2,1,0:T(8,128)} async-done(((f32[16,256,128]{2,1,0:T(8,128)}), f32[16,256,128]{2,1,0:T(8,128)}, u32[]{:S(2)}, u32[]{:S(2)}) %all-to-all-start.4) | async-done | bytes 2097184 | tf_op jit(solution)/shard_map/all_to_all | solution.py:153
  276.7 4.7 %all-to-all-start.2 = ((bf16[16,256,256]{1,2,0:T(8,128)(2,1)}), bf16[16,256,256]{1,2,0:T(8,128)(2,1)S(1)}, u32[]{:S(2)}, u32[]{:S(2)}) async-start(bf16[16,256,256]{1,2,0:T(8,128)(2,1)} %copy.85), calls=%async_computation.2 | async-start | bytes 4194304 | tf_op jit(solution)/shard_map/all_to_all | solution.py:139
  283.8 45.2 %all-to-all-done.2 = bf16[16,256,256]{1,2,0:T(8,128)(2,1)S(1)} async-done(((bf16[16,256,256]{1,2,0:T(8,128)(2,1)}), bf16[16,256,256]{1,2,0:T(8,128)(2,1)S(1)}, u32[]{:S(2)}, u32[]{:S(2)}) %all-to-all-start.2) | async-done | bytes 2097184 | tf_op jit(solution)/shard_map/all_to_all | solution.py:139
  (117 shorter events, 58.9 us)
Async XLA Ops:
  2.0 12.4 %all-to-all-start.1 = ((bf16[256,16,4]{0,2,1:T(4,128)(2,1)}), bf16[256,16,4]{0,2,1:T(4,128)(2,1)S(1)}, u32[]{:S(2)}, u32[]{:S(2)}) async-start(bf16[256,16,4]{0,2,1:T(4,128)(2,1)} %reshape.129), calls=%async_computation.1 | async-start | bytes 65536 | tf_op jit(solution)/shard_map/all_to_all | solution.py:132
  14.4 6.0 %copy-start.15 = (bf16[256,128]{1,0:T(8,128)(2,1)S(1)}, bf16[256,128]{1,0:T(8,128)(2,1)}, u32[]{:S(2)}) copy-start(bf16[256,128]{1,0:T(8,128)(2,1)} %param.8) | copy-start | bytes 196612
  14.4 6.0 %copy-start.16 = (bf16[256,128]{1,0:T(8,128)(2,1)S(1)}, bf16[256,128]{1,0:T(8,128)(2,1)}, u32[]{:S(2)}) copy-start(bf16[256,128]{1,0:T(8,128)(2,1)} %param.9) | copy-start | bytes 196612
  14.4 75.6 %all-to-all-start.3 = ((bf16[256,16,256]{0,2,1:T(8,128)(2,1)}), bf16[256,16,256]{0,2,1:T(8,128)(2,1)S(1)}, u32[]{:S(2)}, u32[]{:S(2)}) async-start(bf16[256,16,256]{0,2,1:T(8,128)(2,1)} %bitcast.187), calls=%async_computation.3 | async-start | bytes 4194304 | tf_op jit(solution)/shard_map/all_to_all | solution.py:130
  20.4 8.2 %collective-permute-start = (bf16[256,128]{1,0:T(8,128)(2,1)S(1)}, bf16[256,128]{1,0:T(8,128)(2,1)S(1)}, u32[]{:S(2)}, u32[]{:S(2)}) collective-permute-start(bf16[256,128]{1,0:T(8,128)(2,1)S(1)} %broadcast_select_fusion.6), channel_id=1, source_target_pairs={{0,2},{2,0},{4,6},{6,4},{8,10},{10,8},{12,14},{14,12},{16,18},{18,... | collective-permute-start | bytes 196616 | tf_op jit(solution)/shard_map/ppermute | solution.py:90
  28.7 5.8 %collective-permute-start.1 = (bf16[512,128]{1,0:T(8,128)(2,1)S(1)}, bf16[512,128]{1,0:T(8,128)(2,1)S(1)}, u32[]{:S(2)}, u32[]{:S(2)}) collective-permute-start(bf16[512,128]{1,0:T(8,128)(2,1)S(1)} %maximum_select_fusion.3), channel_id=1, source_target_pairs={{0,4},{2,6},{4,0},{6,2},{8,12},{10,14},{12,8},{14,10},{16,20},{18,... | collective-permute-start | bytes 393224 | tf_op jit(solution)/shard_map/ppermute | solution.py:90
  34.5 25.5 %collective-permute-start.2 = (bf16[1024,128]{1,0:T(8,128)(2,1)S(1)}, bf16[1024,128]{1,0:T(8,128)(2,1)S(1)}, u32[]{:S(2)}, u32[]{:S(2)}) collective-permute-start(bf16[1024,128]{1,0:T(8,128)(2,1)S(1)} %maximum_select_fusion.2), channel_id=1, source_target_pairs={{0,8},{2,10},{4,12},{6,14},{8,0},{10,2},{12,4},{14,6},{16,24},{18,... | collective-permute-start | bytes 786440 | tf_op jit(solution)/shard_map/ppermute | solution.py:90
  60.2 7.6 %copy-start.14 = (bf16[2048,128]{1,0:T(8,128)(2,1)}, bf16[2048,128]{1,0:T(8,128)(2,1)S(1)}, u32[]{:S(2)}) copy-start(bf16[2048,128]{1,0:T(8,128)(2,1)S(1)} %maximum_select_fusion.1) | copy-start | bytes 1572868
  60.2 28.0 %collective-permute-start.3 = (bf16[2048,128]{1,0:T(8,128)(2,1)S(1)}, bf16[2048,128]{1,0:T(8,128)(2,1)}, u32[]{:S(2)}, u32[]{:S(2)}) collective-permute-start(bf16[2048,128]{1,0:T(8,128)(2,1)S(1)} %maximum_select_fusion.1), channel_id=1, source_target_pairs={{0,16},{2,18},{4,20},{6,22},{8,24},{10,26},{12,28},{14,30},{16,0},... | collective-permute-start | bytes 1572872 | tf_op jit(solution)/shard_map/ppermute | solution.py:90
  90.0 8.4 %copy-start.27 = (f32[64]{0:T(128)S(1)}, f32[64]{0:T(128)}, u32[]{:S(2)}) copy-start(f32[64]{0:T(128)} %param.11) | copy-start | bytes 772
  90.1 8.4 %copy-start.7 = (bf16[256,16,256]{0,2,1:T(8,128)(2,1)}, bf16[256,16,256]{0,2,1:T(8,128)(2,1)S(1)}, u32[]{:S(2)}) copy-start(bf16[256,16,256]{0,2,1:T(8,128)(2,1)S(1)} %all-to-all-done.3) | copy-start | bytes 6291460
  90.1 54.8 %all-to-all-start = ((bf16[256,16,256]{0,2,1:T(8,128)(2,1)}), bf16[256,16,256]{0,2,1:T(8,128)(2,1)}, u32[]{:S(2)}, u32[]{:S(2)}) async-start(bf16[256,16,256]{0,2,1:T(8,128)(2,1)} %bitcast.188), calls=%async_computation | async-start | bytes 4194304 | tf_op jit(solution)/shard_map/all_to_all | solution.py:131
  98.6 2.7 collective-permute-start.4
  99.6 53.7 %copy-start.17 = (f32[4,16,256]{2,1,0:T(8,128)}, f32[4,16,256]{2,1,0:T(8,128)S(1)}, u32[]{:S(2)}) copy-start(f32[4,16,256]{2,1,0:T(8,128)S(1)} %get-tuple-element.36) | copy-start | bytes 196612
  183.5 5.2 %copy-start = (f32[16,4,64,128]{3,2,1,0:T(8,128)}, f32[16,4,64,128]{3,2,1,0:T(8,128)S(1)}, u32[]{:S(2)}) copy-start(f32[16,4,64,128]{3,2,1,0:T(8,128)S(1)} %fusion.8) | copy-start | bytes 6291460
  183.5 5.2 %copy-start.23 = (f32[4,16]{1,0:T(4,128)S(1)}, f32[4,16]{1,0:T(4,128)}, u32[]{:S(2)}) copy-start(f32[4,16]{1,0:T(4,128)} %get-tuple-element.22) | copy-start | bytes 772
  198.0 4.4 %copy-start.11 = (f32[16,256,128,1]{2,1,3,0:T(8,128)S(1)}, f32[16,256,128,1]{2,1,3,0:T(8,128)}, u32[]{:S(2)}) copy-start(f32[16,256,128,1]{2,1,3,0:T(8,128)} %fusion.9) | copy-start | bytes 6291460
  206.3 10.3 %collective-permute-start.5 = (f32[4096,128]{1,0:T(8,128)}, f32[4096,128]{1,0:T(8,128)}, u32[]{:S(2)}, u32[]{:S(2)}) collective-permute-start(f32[4096,128]{1,0:T(8,128)} %bitcast.34), channel_id=1, source_target_pairs={{0,1},{1,0},{2,3},{3,2},{4,5},{5,4},{6,7},{7,6},{8,9},{9,8},{10,11... | collective-permute-start | bytes 6291464 | tf_op jit(solution)/shard_map/ppermute | solution.py:152
  211.4 10.4 %all-to-all-start.5 = ((bf16[16,256,4]{1,2,0:T(4,128)(2,1)}), bf16[16,256,4]{1,2,0:T(4,128)(2,1)S(1)}, u32[]{:S(2)}, u32[]{:S(2)}) async-start(bf16[16,256,4]{1,2,0:T(4,128)(2,1)} %bitcast.40), calls=%async_computation.5 | async-start | bytes 65536 | tf_op jit(solution)/shard_map/all_to_all | solution.py:142
  221.9 7.0 %copy-start.28 = (f32[64]{0:T(128)S(1)}, f32[64]{0:T(128)}, u32[]{:S(2)}) copy-start(f32[64]{0:T(128)} %param.12) | copy-start | bytes 772
  221.9 7.1 %copy-start.3 = (bf16[4096,4,64]{0,2,1:T(8,128)(2,1)S(1)}, bf16[4096,4,64]{0,2,1:T(8,128)(2,1)}, u32[]{:S(2)}) copy-start(bf16[4096,4,64]{0,2,1:T(8,128)(2,1)} %reshape.128) | copy-start | bytes 6291460
  221.9 54.9 %all-to-all-start.4 = ((f32[16,256,128]{2,1,0:T(8,128)}), f32[16,256,128]{2,1,0:T(8,128)}, u32[]{:S(2)}, u32[]{:S(2)}) async-start(f32[16,256,128]{2,1,0:T(8,128)} %bitcast.185), calls=%async_computation.4 | async-start | bytes 4194304 | tf_op jit(solution)/shard_map/all_to_all | solution.py:153
  276.7 52.4 %all-to-all-start.2 = ((bf16[16,256,256]{1,2,0:T(8,128)(2,1)}), bf16[16,256,256]{1,2,0:T(8,128)(2,1)S(1)}, u32[]{:S(2)}, u32[]{:S(2)}) async-start(bf16[16,256,256]{1,2,0:T(8,128)(2,1)} %copy.85), calls=%async_computation.2 | async-start | bytes 4194304 | tf_op jit(solution)/shard_map/all_to_all | solution.py:139
  283.1 48.8 %collective-permute-start.6 = (f32[256,128]{1,0:T(8,128)S(1)}, f32[256,128]{1,0:T(8,128)S(1)}, u32[]{:S(2)}, u32[]{:S(2)}) collective-permute-start(f32[256,128]{1,0:T(8,128)S(1)} %reduce_sum.107), channel_id=1, source_target_pairs={{0,1},{1,0},{2,3},{3,2},{4,5},{5,4},{6,7},{7,6},{8,9},{9,8},{10,11... | collective-permute-start | bytes 393224 | tf_op jit(solution)/shard_map/ppermute | solution.py:155
  (19 other events, 65.1 us)

commit v2 on v1

--- a/solution.py
+++ b/solution.py
@@ -150,8 +150,7 @@
     send = jnp.where(is_first, grad_c_all, grad_b_all)
     keep = jnp.where(is_first, grad_b_all, grad_c_all)
     mine = keep + lax.ppermute(send, "tp", [(0, 1), (1, 0)])
-    parts = lax.all_to_all(mine.reshape(owners, rows, state), "ctx", split_axis=0, concat_axis=0, tiled=True)
-    mine = parts.sum(axis=0)
+    mine = lax.psum_scatter(mine, "ctx", scatter_dimension=0, tiled=True)
     other = lax.ppermute(mine, "tp", [(0, 1), (1, 0)])
     grad_b = jnp.where(is_first, mine, other)
     grad_c = jnp.where(is_first, other, mine)

time: 336 us -> 357 us (1.062)
  the two profiles are of different devices: /device:TPU:12 before, /device:TPU:1 now
where the time goes in v2:
time: 357 us; the launch traced here: 354 us
  waiting for transfers between devices  167 us (47%)
  matrix products  67.5 us (19%)
  starting transfers between devices  55 us (15%)
  local copies, waits for them, and re-layouts  38.5 us (11%)
  between operations  14.8 us (4%)
  other arithmetic  10.6 us (3%)
    reduce_scatter x1, waiting for transfers between devices, local(): mine = lax.psum_scatter(mine, 'ctx', scatter_dimension=0, tiled=True)  80.9 us
    ppermute x4, waiting for transfers between devices, gather_ctx(): theirs = lax.ppermute(have, 'ctx', [(k, k ^ step) for k in range(owners)])  57.8 us
    all_to_all x1, waiting for transfers between devices, local(): lax.all_to_all(g_in, 'ctx', split_axis=1, concat_axis=0, tiled=True)  26 us
    dot_general x2, matrix products, head_forward(): output = jnp.einsum('kij,kjp->kip', scores, x_blocks, precision=precise)  25.5 us
    unnamed x69, local copies, waits for them, and re-layouts  13.8 us
    dot_general x2, matrix products, head_forward(): jnp.einsum('kin,kpn->kip', reading, entering, precision=precise)  11.2 us
    dot_general x3, matrix products, head_forward(): jnp.einsum('kin,kjn->kij', c_blocks, b_blocks, precision=precise)  10.9 us
    dot_general x3, matrix products, head_forward(): states = jnp.einsum('kjp,kjn->kpn', weighted, b_blocks, precision=precise)  10.4 us
  transfers between devices with their start and end apart: 13, of which 8 were waited for; matrix products, arithmetic and copies ran while one was open for 13% of the time, Pallas kernels for 0%

profile of v2, /device:TPU:1, one launch (start us, length us, event | category | flops | bytes accessed | tf_op | source)
XLA Modules:
  0.0 353.9 jit_solution(15920571469047280754)
XLA Ops:
  8.6 7.4 %all-to-all-start.1 = ((bf16[256,16,4]{0,2,1:T(4,128)(2,1)}), bf16[256,16,4]{0,2,1:T(4,128)(2,1)S(1)}, u32[]{:S(2)}, u32[]{:S(2)}) async-start(bf16[256,16,4]{0,2,1:T(4,128)(2,1)} %reshape.126), calls=%async_computation.1 | async-start | bytes 65536 | tf_op jit(solution)/shard_map/all_to_all | solution.py:132
  16.0 4.1 %copy.86 = bf16[256,4096]{0,1:T(8,128)(2,1)} copy(bf16[256,4096]{1,0:T(8,128)(2,1)} %param.7) | data formatting | bytes 4194304 | tf_op args[0]
  22.2 4.3 %all-to-all-start.3 = ((bf16[256,16,256]{0,2,1:T(8,128)(2,1)}), bf16[256,16,256]{0,2,1:T(8,128)(2,1)S(1)}, u32[]{:S(2)}, u32[]{:S(2)}) async-start(bf16[256,16,256]{0,2,1:T(8,128)(2,1)} %bitcast.185), calls=%async_computation.3 | async-start | bytes 4194304 | tf_op jit(solution)/shard_map/all_to_all | solution.py:130
  28.0 6.5 %collective-permute-done = bf16[256,128]{1,0:T(8,128)(2,1)S(1)} collective-permute-done((bf16[256,128]{1,0:T(8,128)(2,1)S(1)}, bf16[256,128]{1,0:T(8,128)(2,1)S(1)}, u32[]{:S(2)}, u32[]{:S(2)}) %collective-permute-start) | collective-permute-done | bytes 65568 | tf_op jit(solution)/shard_map/ppermute | solution.py:90
  36.9 4.5 %collective-permute-done.1 = bf16[512,128]{1,0:T(8,128)(2,1)S(1)} collective-permute-done((bf16[512,128]{1,0:T(8,128)(2,1)S(1)}, bf16[512,128]{1,0:T(8,128)(2,1)S(1)}, u32[]{:S(2)}, u32[]{:S(2)}) %collective-permute-start.1) | collective-permute-done | bytes 131104 | tf_op jit(solution)/shard_map/ppermute | solution.py:90
  41.6 23.2 %collective-permute-done.2 = bf16[1024,128]{1,0:T(8,128)(2,1)S(1)} collective-permute-done((bf16[1024,128]{1,0:T(8,128)(2,1)S(1)}, bf16[1024,128]{1,0:T(8,128)(2,1)S(1)}, u32[]{:S(2)}, u32[]{:S(2)}) %collective-permute-start.2) | collective-permute-done | bytes 262176 | tf_op jit(solution)/shard_map/ppermute | solution.py:90
  65.0 4.2 %collective-permute-start.3 = (bf16[2048,128]{1,0:T(8,128)(2,1)S(1)}, bf16[2048,128]{1,0:T(8,128)(2,1)}, u32[]{:S(2)}, u32[]{:S(2)}) collective-permute-start(bf16[2048,128]{1,0:T(8,128)(2,1)S(1)} %maximum_select_fusion.1), channel_id=1, source_target_pairs={{0,16},{2,18},{4,20},{6,22},{8,24},{10,26},{12,28},{14,30},{16,0},... | collective-permute-start | bytes 1572872 | tf_op jit(solution)/shard_map/ppermute | solution.py:90
  69.2 4.1 %copy.73 = bf16[256,4096]{0,1:T(8,128)(2,1)} copy(bf16[256,4096]{1,0:T(8,128)(2,1)} %param.13) | data formatting | bytes 4194304 | tf_op args[6]
  73.3 23.6 %collective-permute-done.3 = bf16[2048,128]{1,0:T(8,128)(2,1)} collective-permute-done((bf16[2048,128]{1,0:T(8,128)(2,1)S(1)}, bf16[2048,128]{1,0:T(8,128)(2,1)}, u32[]{:S(2)}, u32[]{:S(2)}) %collective-permute-start.3) | collective-permute-done | bytes 524320 | tf_op jit(solution)/shard_map/ppermute | solution.py:90
  98.7 5.2 %all-to-all-start = ((bf16[256,16,256]{0,2,1:T(8,128)(2,1)}), bf16[256,16,256]{0,2,1:T(8,128)(2,1)}, u32[]{:S(2)}, u32[]{:S(2)}) async-start(bf16[256,16,256]{0,2,1:T(8,128)(2,1)} %bitcast.186), calls=%async_computation | async-start | bytes 4194304 | tf_op jit(solution)/shard_map/all_to_all | solution.py:131
  119.0 26.0 %all-to-all-done = bf16[256,16,256]{0,2,1:T(8,128)(2,1)} async-done(((bf16[256,16,256]{0,2,1:T(8,128)(2,1)}), bf16[256,16,256]{0,2,1:T(8,128)(2,1)}, u32[]{:S(2)}, u32[]{:S(2)}) %all-to-all-start) | async-done | bytes 2097184 | tf_op jit(solution)/shard_map/all_to_all | solution.py:131
  145.1 4.1 %copy.74 = bf16[16,256,1,256]{1,0,3,2:T(8,128)(2,1)} copy(bf16[16,256,1,256]{1,3,0,2:T(8,128)(2,1)} %bitcast.2) | data formatting | bytes 4194304 | tf_op jit(solution)/shard_map/all_to_all | solution.py:131
  149.2 4.3 %reshape.125 = bf16[4096,4,64]{0,2,1:T(8,128)(2,1)} reshape(bf16[16,256,1,256]{1,0,3,2:T(8,128)(2,1)} %copy.74) | data formatting | bytes 4194304 | tf_op jit(solution)/shard_map/reshape | solution.py:131
  153.5 5.8 %multiply_reduce_fusion.4 = (f32[4,16]{1,0:T(4,128)}, f32[4,16,64,128]{3,2,1,0:T(8,128)S(1)}) fusion(f32[16,256,128]{1,2,0:T(8,128)} %copy.76, f32[4,16,256]{2,1,0:T(8,128)S(1)} %get-tuple-element.36, bf16[4,8,16,8,256]{4,3,2,1,0:T(8,128)(2,1)} %bitcast.176), kind=kOutput, calls=%fused_computation.40 | convolution fusion | flops 808452032 | bytes 6357248 | tf_op jit(solution)/shard_map/transpose(jvp(vmap(kin,kpn->kip)))/dot_general | solution.py:51
  165.3 16.2 %fusion.5 = (f32[4,16,256]{2,1,0:T(8,128)}, f32[4,16,256]{2,1,0:T(8,128)}, f32[4,16,256]{2,1,0:T(8,128)S(1)}, f32[16,256,256]{2,1,0:T(8,128)}, f32[4,16,256,256]{3,2,1,0:T(8,128)}) fusion(f32[4,16,256]{2,1,0:T(8,128)S(1)} %bitcast.199, f32[4,16,256]{2,1,0:T(8,128)S(1)} %get-tuple-element.37, f32[16,256,256]{2,1,0:T(8,128)S(1)} %copy-done.9, ...), kind=kOutput, calls=%fused_computation.9 | convolution fusion | flops 594493440 | bytes 29753344 | tf_op jit(solution)/shard_map/transpose(jvp(vmap(kij,kjp->kip)))/dot_general | solution.py:35
  183.6 5.2 %fusion.9 = f32[16,256,128,1]{2,1,3,0:T(8,128)} fusion(f32[4,16,256]{2,0,1:T(4,128)S(1)} %copy.75, f32[16,4,64,128]{3,0,2,1:T(8,128)S(1)} %fusion.44, bf16[4,8,16,8,256]{4,3,2,1,0:T(8,128)(2,1)S(1)} %bitcast.171), kind=kOutput, calls=%fused_computation.17 | convolution fusion | flops 807403520 | bytes 6356992 | tf_op jit(solution)/shard_map/transpose(jvp(vmap(kjp,kjn->kpn)))/dot_general | solution.py:38
  188.8 4.2 %fusion.111 = (f32[4,16]{1,0:T(4,128)}, f32[4,16]{1,0:T(4,128)}) fusion(f32[4,16]{1,0:T(4,128)S(1)} %get-tuple-element.38, f32[4,16]{1,0:T(4,128)S(1)} %get-tuple-element.23, f32[16,4,64,128]{3,2,1,0:T(8,128)S(1)} %fusion.8, f32[4,16,64,128]{3,2,1,0:T(8,128)S(1)} %get-tuple-element.42, pred[16,16]{1,0:T(8,128)(4,1)S(1)} %iota_compare_fusion.6), kind=kOutput, calls=%fused_computation.134 | convolution fusion | flops 50337664 | bytes 4195584 | tf_op jit(solution)/shard_map/transpose(jvp(vmap(kj,jpn->kpn)))/dot_general | solution.py:47
  195.1 5.3 %multiply_reduce_fusion.2 = (f32[4,16,256]{2,1,0:T(8,128)}, f32[16,256,128]{1,2,0:T(8,128)}) fusion(f32[16,256,128]{1,2,0:T(8,128)S(1)} %copy-done.10, f32[4,16,256]{2,1,0:T(8,128)S(1)} %copy-done.16, f32[4,16,64,128]{3,1,2,0:T(8,128)S(1)} %fusion.47, bf16[4,8,16,8,256]{4,3,2,1,0:T(8,128)(2,1)S(1)} %bitcast.178), kind=kOutput, calls=%fused_computation.10 | convolution fusion | flops 813154304 | bytes 8519680 | tf_op jit(solution)/shard_map/transpose(jvp(vmap(kin,kpn->kip)))/dot_general | solution.py:51
  206.8 4.5 %broadcast_select_fusion.1 = (f32[16,256,128]{2,1,0:T(8,128)}, f32[16,256,128]{2,1,0:T(8,128)}) fusion(f32[16,256,128]{2,1,0:T(8,128)S(1)} %convolution_add_fusion, pred[]{:T(512)S(6)} %eq.35, f32[16,256,256]{2,1,0:T(8,128)S(1)} %copy-done.2, bf16[16,256,128]{2,1,0:T(8,128)(2,1)S(1)} %bitcast.183, f32[16,256,128,1]{2,1,3,0:T(8,128)S(1)} %copy-done.8), kind=kOutput, calls=%fused_computation.70 | convolution fusion | flops 806879232 | bytes 13631489 | tf_op jit(solution)/shard_map/transpose(jvp(vmap(kin,kjn->kij)))/dot_general | solution.py:31
  215.2 10.0 %all-to-all-start.4 = ((bf16[16,256,4]{1,2,0:T(4,128)(2,1)}), bf16[16,256,4]{1,2,0:T(4,128)(2,1)S(1)}, u32[]{:S(2)}, u32[]{:S(2)}) async-start(bf16[16,256,4]{1,2,0:T(4,128)(2,1)} %bitcast.39), calls=%async_computation.5 | async-start | bytes 65536 | tf_op jit(solution)/shard_map/all_to_all | solution.py:142
  225.2 9.3 %fusion.12 = f32[16,4,8,8,256]{4,3,2,1,0:T(8,128)S(1)} fusion(f32[16,4,64,256]{3,2,1,0:T(8,128)} %get-tuple-element.40, f32[4,16,256]{2,0,1:T(4,128)S(1)} %copy.75, bf16[4,8,16,8,256]{4,3,2,1,0:T(8,128)(2,1)S(1)} %bitcast.179, f32[4,16,256,256]{3,2,1,0:T(8,128)} %get-tuple-element.24), kind=kOutput, calls=%fused_computation.21 | convolution fusion | flops 1612709888 | bytes 27328512 | tf_op jit(solution)/shard_map/transpose(jvp(vmap(kij,kjp->kip)))/dot_general | solution.py:35
  246.2 6.3 %all-to-all-start.2 = ((bf16[16,256,256]{1,2,0:T(8,128)(2,1)}), bf16[16,256,256]{1,2,0:T(8,128)(2,1)S(1)}, u32[]{:S(2)}, u32[]{:S(2)}) async-start(bf16[16,256,256]{1,2,0:T(8,128)(2,1)} %copy.85), calls=%async_computation.2 | async-start | bytes 4194304 | tf_op jit(solution)/shard_map/all_to_all | solution.py:139
  252.6 80.9 %reduce-scatter.2.cloned.1.call-done = f32[256,128]{1,0:T(8,128)} async-done(((f32[4096,128]{1,0:T(8,128)}), f32[256,128]{1,0:T(8,128)}) %reduce-scatter.2.cloned.1.call-update) | async-done | bytes 131088 | tf_op jit(solution)/shard_map/reduce_scatter | solution.py:153
  333.5 9.0 %collective-permute-start.6 = (f32[256,128]{1,0:T(8,128)}, f32[256,128]{1,0:T(8,128)S(1)}, u32[]{:S(2)}, u32[]{:S(2)}) collective-permute-start(f32[256,128]{1,0:T(8,128)} %reduce-scatter.2.cloned.1.call-done), channel_id=1, source_target_pairs={{0,1},{1,0},{2,3},{3,2},{4,5},{5,4},{6,7},{7,6},{8,9},{9,8},{10,11... | collective-permute-start | bytes 393224 | tf_op jit(solution)/shard_map/ppermute | solution.py:154
  (119 shorter events, 60.6 us)
Async XLA Ops:
  8.6 13.7 %all-to-all-start.1 = ((bf16[256,16,4]{0,2,1:T(4,128)(2,1)}), bf16[256,16,4]{0,2,1:T(4,128)(2,1)S(1)}, u32[]{:S(2)}, u32[]{:S(2)}) async-start(bf16[256,16,4]{0,2,1:T(4,128)(2,1)} %reshape.126), calls=%async_computation.1 | async-start | bytes 65536 | tf_op jit(solution)/shard_map/all_to_all | solution.py:132
  22.2 76.5 %all-to-all-start.3 = ((bf16[256,16,256]{0,2,1:T(8,128)(2,1)}), bf16[256,16,256]{0,2,1:T(8,128)(2,1)S(1)}, u32[]{:S(2)}, u32[]{:S(2)}) async-start(bf16[256,16,256]{0,2,1:T(8,128)(2,1)} %bitcast.185), calls=%async_computation.3 | async-start | bytes 4194304 | tf_op jit(solution)/shard_map/all_to_all | solution.py:130
  26.6 7.9 %collective-permute-start = (bf16[256,128]{1,0:T(8,128)(2,1)S(1)}, bf16[256,128]{1,0:T(8,128)(2,1)S(1)}, u32[]{:S(2)}, u32[]{:S(2)}) collective-permute-start(bf16[256,128]{1,0:T(8,128)(2,1)S(1)} %broadcast_select_fusion.6), channel_id=1, source_target_pairs={{0,2},{2,0},{4,6},{6,4},{8,10},{10,8},{12,14},{14,12},{16,18},{18,... | collective-permute-start | bytes 196616 | tf_op jit(solution)/shard_map/ppermute | solution.py:90
  34.5 6.9 %collective-permute-start.1 = (bf16[512,128]{1,0:T(8,128)(2,1)S(1)}, bf16[512,128]{1,0:T(8,128)(2,1)S(1)}, u32[]{:S(2)}, u32[]{:S(2)}) collective-permute-start(bf16[512,128]{1,0:T(8,128)(2,1)S(1)} %maximum_select_fusion.3), channel_id=1, source_target_pairs={{0,4},{2,6},{4,0},{6,2},{8,12},{10,14},{12,8},{14,10},{16,20},{18,... | collective-permute-start | bytes 393224 | tf_op jit(solution)/shard_map/ppermute | solution.py:90
  41.5 23.3 %collective-permute-start.2 = (bf16[1024,128]{1,0:T(8,128)(2,1)S(1)}, bf16[1024,128]{1,0:T(8,128)(2,1)S(1)}, u32[]{:S(2)}, u32[]{:S(2)}) collective-permute-start(bf16[1024,128]{1,0:T(8,128)(2,1)S(1)} %maximum_select_fusion.2), channel_id=1, source_target_pairs={{0,8},{2,10},{4,12},{6,14},{8,0},{10,2},{12,4},{14,6},{16,24},{18,... | collective-permute-start | bytes 786440 | tf_op jit(solution)/shard_map/ppermute | solution.py:90
  65.0 8.3 %copy-start.11 = (bf16[2048,128]{1,0:T(8,128)(2,1)}, bf16[2048,128]{1,0:T(8,128)(2,1)S(1)}, u32[]{:S(2)}) copy-start(bf16[2048,128]{1,0:T(8,128)(2,1)S(1)} %maximum_select_fusion.1) | copy-start | bytes 1572868
  65.0 31.9 %collective-permute-start.3 = (bf16[2048,128]{1,0:T(8,128)(2,1)S(1)}, bf16[2048,128]{1,0:T(8,128)(2,1)}, u32[]{:S(2)}, u32[]{:S(2)}) collective-permute-start(bf16[2048,128]{1,0:T(8,128)(2,1)S(1)} %maximum_select_fusion.1), channel_id=1, source_target_pairs={{0,16},{2,18},{4,20},{6,22},{8,24},{10,26},{12,28},{14,30},{16,0},... | collective-permute-start | bytes 1572872 | tf_op jit(solution)/shard_map/ppermute | solution.py:90
  98.7 46.4 %all-to-all-start = ((bf16[256,16,256]{0,2,1:T(8,128)(2,1)}), bf16[256,16,256]{0,2,1:T(8,128)(2,1)}, u32[]{:S(2)}, u32[]{:S(2)}) async-start(bf16[256,16,256]{0,2,1:T(8,128)(2,1)} %bitcast.186), calls=%async_computation | async-start | bytes 4194304 | tf_op jit(solution)/shard_map/all_to_all | solution.py:131
  104.6 4.5 %collective-permute-start.4 = (bf16[4096,128]{1,0:T(8,128)(2,1)S(1)}, bf16[4096,128]{1,0:T(8,128)(2,1)S(1)}, u32[]{:S(2)}, u32[]{:S(2)}) collective-permute-start(bf16[4096,128]{1,0:T(8,128)(2,1)S(1)} %maximum_select_fusion), channel_id=1, source_target_pairs={{0,1},{1,0},{2,3},{3,2},{4,5},{5,4},{6,7},{7,6},{8,9},{9,8},{10,11... | collective-permute-start | bytes 3145736 | tf_op jit(solution)/shard_map/ppermute | solution.py:110
  107.8 45.6 %copy-start.15 = (f32[4,16,256]{2,1,0:T(8,128)}, f32[4,16,256]{2,1,0:T(8,128)S(1)}, u32[]{:S(2)}) copy-start(f32[4,16,256]{2,1,0:T(8,128)S(1)} %get-tuple-element.36) | copy-start | bytes 196612
  206.8 7.0 %copy-start.22 = (f32[4,16]{1,0:T(4,128)S(1)}, f32[4,16]{1,0:T(4,128)}, u32[]{:S(2)}) copy-start(f32[4,16]{1,0:T(4,128)} %get-tuple-element.31) | copy-start | bytes 772
  206.8 7.0 %copy-start.23 = (f32[4,16]{1,0:T(4,128)S(1)}, f32[4,16]{1,0:T(4,128)}, u32[]{:S(2)}) copy-start(f32[4,16]{1,0:T(4,128)} %get-tuple-element.20) | copy-start | bytes 772
  206.8 7.0 %copy-start.24 = (f32[4,16]{1,0:T(4,128)S(1)}, f32[4,16]{1,0:T(4,128)}, u32[]{:S(2)}) copy-start(f32[4,16]{1,0:T(4,128)} %get-tuple-element.21) | copy-start | bytes 772
  206.8 7.0 %copy-start.30 = (f32[4,16]{1,0:T(4,128)S(1)}, f32[4,16]{1,0:T(4,128)}, u32[]{:S(2)}) copy-start(f32[4,16]{1,0:T(4,128)} %get-tuple-element.41) | copy-start | bytes 772
  206.8 7.3 %copy-start.17 = (f32[4,16,256]{2,1,0:T(8,128)S(1)}, f32[4,16,256]{2,1,0:T(8,128)}, u32[]{:S(2)}) copy-start(f32[4,16,256]{2,1,0:T(8,128)} %get-tuple-element.14) | copy-start | bytes 196612
  206.8 7.3 %copy-start.18 = (f32[4,16,256]{2,1,0:T(8,128)S(1)}, f32[4,16,256]{2,1,0:T(8,128)}, u32[]{:S(2)}) copy-start(f32[4,16,256]{2,1,0:T(8,128)} %get-tuple-element.15) | copy-start | bytes 196612
  206.8 7.3 %copy-start.19 = (f32[4,16,256]{2,1,0:T(8,128)S(1)}, f32[4,16,256]{2,1,0:T(8,128)}, u32[]{:S(2)}) copy-start(f32[4,16,256]{2,1,0:T(8,128)} %get-tuple-element.18) | copy-start | bytes 196612
  206.8 7.6 %copy-start.26 = (f32[4]{0:T(128)S(1)}, f32[4]{0:T(128)}, u32[]{:S(2)}) copy-start(f32[4]{0:T(128)} %copy-done.25) | copy-start | bytes 52
  206.8 18.4 %copy-start.1 = (bf16[4096,4,64]{0,2,1:T(8,128)(2,1)S(1)}, bf16[4096,4,64]{0,2,1:T(8,128)(2,1)}, u32[]{:S(2)}) copy-start(bf16[4096,4,64]{0,2,1:T(8,128)(2,1)} %reshape.125) | copy-start | bytes 6291460
  211.4 25.6 %collective-permute-start.5 = (f32[4096,128]{1,0:T(8,128)}, f32[4096,128]{1,0:T(8,128)}, u32[]{:S(2)}, u32[]{:S(2)}) collective-permute-start(f32[4096,128]{1,0:T(8,128)} %bitcast.34), channel_id=1, source_target_pairs={{0,1},{1,0},{2,3},{3,2},{4,5},{5,4},{6,7},{7,6},{8,9},{9,8},{10,11... | collective-permute-start | bytes 6291464 | tf_op jit(solution)/shard_map/ppermute | solution.py:152
  215.2 31.1 %all-to-all-start.4 = ((bf16[16,256,4]{1,2,0:T(4,128)(2,1)}), bf16[16,256,4]{1,2,0:T(4,128)(2,1)S(1)}, u32[]{:S(2)}, u32[]{:S(2)}) async-start(bf16[16,256,4]{1,2,0:T(4,128)(2,1)} %bitcast.39), calls=%async_computation.5 | async-start | bytes 65536 | tf_op jit(solution)/shard_map/all_to_all | solution.py:142
  225.2 108.3 %reduce-scatter.2.cloned.1.call-start = ((), (), s32[]{:S(2)}) async-start(), calls=%async_computation.6 | async-start | bytes 2228224 | tf_op jit(solution)/shard_map/reduce_scatter | solution.py:153
  246.2 96.9 %all-to-all-start.2 = ((bf16[16,256,256]{1,2,0:T(8,128)(2,1)}), bf16[16,256,256]{1,2,0:T(8,128)(2,1)S(1)}, u32[]{:S(2)}, u32[]{:S(2)}) async-start(bf16[16,256,256]{1,2,0:T(8,128)(2,1)} %copy.85), calls=%async_computation.2 | async-start | bytes 4194304 | tf_op jit(solution)/shard_map/all_to_all | solution.py:139
  333.5 12.5 %collective-permute-start.6 = (f32[256,128]{1,0:T(8,128)}, f32[256,128]{1,0:T(8,128)S(1)}, u32[]{:S(2)}, u32[]{:S(2)}) collective-permute-start(f32[256,128]{1,0:T(8,128)} %reduce-scatter.2.cloned.1.call-done), channel_id=1, source_target_pairs={{0,1},{1,0},{2,3},{3,2},{4,5},{5,4},{6,7},{7,6},{8,9},{9,8},{10,11... | collective-permute-start | bytes 393224 | tf_op jit(solution)/shard_map/ppermute | solution.py:154
  (20 other events, 72.9 us)
Sparse Core Ops, SparseCore 0:
  240.2 93.2 reduce-scatter.1

commit v3 on v2

--- a/solution.py
+++ b/solution.py
@@ -77,7 +77,7 @@
     _, pullback = jax.vjp(forward, x_heads, b_rows, c_rows, raw_heads)
     grad_xh, grad_b_all, grad_c_all, grad_raw = pullback(g_heads)
     x_back = grad_xh.transpose(1, 0, 2).reshape(length, heads * head_width).astype(jnp.bfloat16)
-    raw_back = grad_raw.T.astype(jnp.bfloat16)
+    raw_back = grad_raw.T
     return x_back, raw_back, grad_b_all, grad_c_all
 
 
@@ -138,19 +138,28 @@
         x_parts.append(
             lax.all_to_all(x_back, "ctx", split_axis=0, concat_axis=1, tiled=True).reshape(rows, owners, 1, width)
         )
-        raw_parts.append(
-            lax.all_to_all(raw_back, "ctx", split_axis=0, concat_axis=1, tiled=True).reshape(rows, owners, 1, per_chunk)
-        )
+        raw_parts.append(raw_back)
         grad_b_all = gb if grad_b_all is None else grad_b_all + gb
         grad_c_all = gc if grad_c_all is None else grad_c_all + gc
     grad_x = jnp.concatenate(x_parts, axis=2).reshape(rows, owners * per_owner * head_width)
-    grad_dt = jnp.concatenate(raw_parts, axis=2).reshape(rows, heads_here)
+    raw_all = jnp.concatenate(raw_parts, axis=1)
 
     is_first = half == 0
     send = jnp.where(is_first, grad_c_all, grad_b_all)
     keep = jnp.where(is_first, grad_b_all, grad_c_all)
     mine = keep + lax.ppermute(send, "tp", [(0, 1), (1, 0)])
-    mine = lax.psum_scatter(mine, "ctx", scatter_dimension=0, tiled=True)
+    steps_back = raw_all.reshape(owners, rows, per_owner).transpose(0, 2, 1)
+    extra = (per_owner * rows) // state
+    if extra * state == per_owner * rows:
+        packed = jnp.concatenate([mine.reshape(owners, rows, state), steps_back.reshape(owners, extra, state)], axis=1)
+        parts = lax.all_to_all(packed, "ctx", split_axis=0, concat_axis=0, tiled=True)
+        mine = parts[:, :rows, :].sum(axis=0)
+        got_dt = parts[:, rows:, :].reshape(owners, per_owner, rows)
+    else:
+        parts = lax.all_to_all(mine.reshape(owners, rows, state), "ctx", split_axis=0, concat_axis=0, tiled=True)
+        mine = parts.sum(axis=0)
+        got_dt = lax.all_to_all(steps_back, "ctx", split_axis=0, concat_axis=0, tiled=True)
+    grad_dt = got_dt.transpose(2, 0, 1).reshape(rows, heads_here).astype(jnp.bfloat16)
     other = lax.ppermute(mine, "tp", [(0, 1), (1, 0)])
     grad_b = jnp.where(is_first, mine, other)
     grad_c = jnp.where(is_first, other, mine)

time: 357 us -> 333 us (0.933)
  the two profiles are of different devices: /device:TPU:1 before, /device:TPU:12 now
where the time goes in v3:
time: 333 us; the launch traced here: 330 us
  waiting for transfers between devices  173 us (52%)
  matrix products  65.9 us (20%)
  starting transfers between devices  41.6 us (12%)
  local copies, waits for them, and re-layouts  37.9 us (11%)
  other arithmetic  9.84 us (3%)
    ppermute x4, waiting for transfers between devices, gather_ctx(): theirs = lax.ppermute(have, 'ctx', [(k, k ^ step) for k in range(owners)])  54.9 us
    all_to_all x1, waiting for transfers between devices, local(): lax.all_to_all(x_back, 'ctx', split_axis=0, concat_axis=1, tiled=True)  46.1 us
    all_to_all x1, waiting for transfers between devices, local(): lax.all_to_all(packed, 'ctx', split_axis=0, concat_axis=0, tiled=True)  36.7 us
    all_to_all x1, waiting for transfers between devices, local(): lax.all_to_all(g_in, 'ctx', split_axis=1, concat_axis=0, tiled=True)  33.6 us
    dot_general x2, matrix products, head_forward(): output = jnp.einsum('kij,kjp->kip', scores, x_blocks, precision=precise)  25.2 us
    unnamed x67, local copies, waits for them, and re-layouts  14.5 us
    dot_general x2, matrix products, head_forward(): jnp.einsum('kin,kpn->kip', reading, entering, precision=precise)  11 us
    dot_general x3, matrix products, head_forward(): states = jnp.einsum('kjp,kjn->kpn', weighted, b_blocks, precision=precise)  10.5 us
  transfers between devices with their start and end apart: 12, of which 9 were waited for; matrix products, arithmetic and copies ran while one was open for 14% of the time, Pallas kernels for 0%

profile of v3, /device:TPU:12, one launch (start us, length us, event | category | flops | bytes accessed | tf_op | source)
XLA Modules:
  0.0 329.9 jit_solution(7301412444082762005)
XLA Ops:
  2.0 7.2 %all-to-all-start.1 = ((bf16[256,16,4]{0,2,1:T(4,128)(2,1)}), bf16[256,16,4]{0,2,1:T(4,128)(2,1)S(1)}, u32[]{:S(2)}, u32[]{:S(2)}) async-start(bf16[256,16,4]{0,2,1:T(4,128)(2,1)} %reshape.136), calls=%async_computation.1 | async-start | bytes 65536 | tf_op jit(solution)/shard_map/all_to_all | solution.py:132
  9.2 4.1 %copy.83 = bf16[256,4096]{0,1:T(8,128)(2,1)} copy(bf16[256,4096]{1,0:T(8,128)(2,1)} %param.7) | data formatting | bytes 4194304 | tf_op args[0]
  14.4 5.9 %all-to-all-start.3 = ((bf16[256,16,256]{0,2,1:T(8,128)(2,1)}), bf16[256,16,256]{0,2,1:T(8,128)(2,1)S(1)}, u32[]{:S(2)}, u32[]{:S(2)}) async-start(bf16[256,16,256]{0,2,1:T(8,128)(2,1)} %bitcast.189), calls=%async_computation.3 | async-start | bytes 4194304 | tf_op jit(solution)/shard_map/all_to_all | solution.py:130
  21.9 6.7 %collective-permute-done = bf16[256,128]{1,0:T(8,128)(2,1)S(1)} collective-permute-done((bf16[256,128]{1,0:T(8,128)(2,1)S(1)}, bf16[256,128]{1,0:T(8,128)(2,1)S(1)}, u32[]{:S(2)}, u32[]{:S(2)}) %collective-permute-start) | collective-permute-done | bytes 65568 | tf_op jit(solution)/shard_map/ppermute | solution.py:90
  29.5 4.9 %collective-permute-done.1 = bf16[512,128]{1,0:T(8,128)(2,1)S(1)} collective-permute-done((bf16[512,128]{1,0:T(8,128)(2,1)S(1)}, bf16[512,128]{1,0:T(8,128)(2,1)S(1)}, u32[]{:S(2)}, u32[]{:S(2)}) %collective-permute-start.1) | collective-permute-done | bytes 131104 | tf_op jit(solution)/shard_map/ppermute | solution.py:90
  37.2 22.8 %collective-permute-done.2 = bf16[1024,128]{1,0:T(8,128)(2,1)S(1)} collective-permute-done((bf16[1024,128]{1,0:T(8,128)(2,1)S(1)}, bf16[1024,128]{1,0:T(8,128)(2,1)S(1)}, u32[]{:S(2)}, u32[]{:S(2)}) %collective-permute-start.2) | collective-permute-done | bytes 262176 | tf_op jit(solution)/shard_map/ppermute | solution.py:90
  63.7 4.1 %copy.70 = bf16[256,4096]{0,1:T(8,128)(2,1)} copy(bf16[256,4096]{1,0:T(8,128)(2,1)} %param.13) | data formatting | bytes 4194304 | tf_op args[6]
  67.8 20.4 %collective-permute-done.3 = bf16[2048,128]{1,0:T(8,128)(2,1)} collective-permute-done((bf16[2048,128]{1,0:T(8,128)(2,1)S(1)}, bf16[2048,128]{1,0:T(8,128)(2,1)}, u32[]{:S(2)}, u32[]{:S(2)}) %collective-permute-start.3) | collective-permute-done | bytes 524320 | tf_op jit(solution)/shard_map/ppermute | solution.py:90
  90.1 8.3 %all-to-all-start = ((bf16[256,16,256]{0,2,1:T(8,128)(2,1)}), bf16[256,16,256]{0,2,1:T(8,128)(2,1)}, u32[]{:S(2)}, u32[]{:S(2)}) async-start(bf16[256,16,256]{0,2,1:T(8,128)(2,1)} %bitcast.190), calls=%async_computation | async-start | bytes 4194304 | tf_op jit(solution)/shard_map/all_to_all | solution.py:131
  111.3 33.6 %all-to-all-done = bf16[256,16,256]{0,2,1:T(8,128)(2,1)} async-done(((bf16[256,16,256]{0,2,1:T(8,128)(2,1)}), bf16[256,16,256]{0,2,1:T(8,128)(2,1)}, u32[]{:S(2)}, u32[]{:S(2)}) %all-to-all-start) | async-done | bytes 2097184 | tf_op jit(solution)/shard_map/all_to_all | solution.py:131
  144.9 4.1 %copy.71 = bf16[16,256,1,256]{1,0,3,2:T(8,128)(2,1)} copy(bf16[16,256,1,256]{1,3,0,2:T(8,128)(2,1)} %bitcast.2) | data formatting | bytes 4194304 | tf_op jit(solution)/shard_map/all_to_all | solution.py:131
  149.0 4.2 %reshape.135 = bf16[4096,4,64]{0,2,1:T(8,128)(2,1)} reshape(bf16[16,256,1,256]{1,0,3,2:T(8,128)(2,1)} %copy.71) | data formatting | bytes 4194304 | tf_op jit(solution)/shard_map/reshape | solution.py:131
  153.2 5.9 %multiply_reduce_fusion.4 = (f32[4,16]{1,0:T(4,128)}, f32[4,16,64,128]{3,2,1,0:T(8,128)S(1)}) fusion(f32[16,256,128]{1,2,0:T(8,128)} %copy.73, f32[4,16,256]{2,1,0:T(8,128)S(1)} %get-tuple-element.36, bf16[4,8,16,8,256]{4,3,2,1,0:T(8,128)(2,1)} %bitcast.179), kind=kOutput, calls=%fused_computation.42 | convolution fusion | flops 808452032 | bytes 6357248 | tf_op jit(solution)/shard_map/transpose(jvp(vmap(kin,kpn->kip)))/dot_general | solution.py:51
  161.1 4.0 %fusion.10 = (f32[4,16,256]{2,0,1:T(4,128)S(1)}, f32[16,4,64,256]{3,2,1,0:T(8,128)}) fusion(bf16[4,8,16,8,256]{4,3,2,1,0:T(8,128)(2,1)S(1)} %bitcast.171, bf16[16,256,128,1]{2,1,3,0:T(8,128)(2,1)S(1)} %bitcast.176, f32[16,4,64,128]{3,0,2,1:T(8,128)S(1)} %fusion.44), kind=kOutput, calls=%fused_computation.18 | convolution fusion | flops 808435712 | bytes 9502720 | tf_op jit(solution)/shard_map/transpose(jvp(vmap(kjp,kjn->kpn)))/dot_general | solution.py:38
  165.2 16.2 %fusion.5 = (f32[4,16,256]{2,1,0:T(8,128)}, f32[4,16,256]{2,1,0:T(8,128)}, f32[4,16,256]{2,1,0:T(8,128)S(1)}, f32[16,256,256]{2,1,0:T(8,128)}, f32[4,16,256,256]{3,2,1,0:T(8,128)}) fusion(f32[4,16,256]{2,1,0:T(8,128)S(1)} %bitcast.204, f32[4,16,256]{2,1,0:T(8,128)S(1)} %get-tuple-element.37, f32[16,256,256]{2,1,0:T(8,128)S(1)} %copy-done.12, ...), kind=kOutput, calls=%fused_computation.9 | convolution fusion | flops 594493440 | bytes 29753344 | tf_op jit(solution)/shard_map/transpose(jvp(vmap(kij,kjp->kip)))/dot_general | solution.py:35
  182.2 5.2 %fusion.9 = f32[16,256,128,1]{2,1,3,0:T(8,128)} fusion(f32[4,16,256]{2,0,1:T(4,128)S(1)} %copy.72, f32[16,4,64,128]{3,0,2,1:T(8,128)S(1)} %fusion.44, bf16[4,8,16,8,256]{4,3,2,1,0:T(8,128)(2,1)S(1)} %bitcast.173), kind=kOutput, calls=%fused_computation.17 | convolution fusion | flops 807403520 | bytes 6356992 | tf_op jit(solution)/shard_map/transpose(jvp(vmap(kjp,kjn->kpn)))/dot_general | solution.py:38
  192.0 5.1 %multiply_reduce_fusion.3 = (f32[16,256,128]{1,2,0:T(8,128)}, f32[4,16,256]{2,1,0:T(8,128)}) fusion(f32[4,16,256]{2,1,0:T(8,128)S(1)} %copy-done.18, f32[16,256,128]{1,2,0:T(8,128)S(1)} %copy-done.13, f32[4,16,64,128]{3,1,2,0:T(8,128)S(1)} %fusion.47, bf16[4,8,16,8,256]{4,3,2,1,0:T(8,128)(2,1)S(1)} %bitcast.181), kind=kOutput, calls=%fused_computation.11 | convolution fusion | flops 813154304 | bytes 8519680 | tf_op jit(solution)/shard_map/transpose(jvp(vmap(kin,kpn->kip)))/dot_general | solution.py:51
  203.7 3.8 %broadcast_select_fusion.1 = (f32[16,256,128]{2,1,0:T(8,128)S(1)}, f32[16,256,128]{2,1,0:T(8,128)}) fusion(f32[16,256,128]{2,1,0:T(8,128)S(1)} %convolution_add_fusion, pred[]{:T(512)S(6)} %eq.35, f32[16,256,256]{2,1,0:T(8,128)S(1)} %copy-done.4, bf16[16,256,128]{2,1,0:T(8,128)(2,1)S(1)} %bitcast.186, f32[16,256,128,1]{2,1,3,0:T(8,128)S(1)} %copy-done.11), kind=kOutput, calls=%fused_computation.72 | convolution fusion | flops 806879232 | bytes 13631489 | tf_op jit(solution)/shard_map/transpose(jvp(vmap(kin,kjn->kij)))/dot_general | solution.py:31
  207.7 3.7 %fusion.110 = (f32[4,16]{1,0:T(4,128)S(1)}, f32[4,16]{1,0:T(4,128)S(1)}) fusion(f32[4,16]{1,0:T(4,128)S(1)} %get-tuple-element.38, f32[4,16]{1,0:T(4,128)S(1)} %get-tuple-element.23, f32[16,4,64,128]{3,2,1,0:T(8,128)S(1)} %copy-done.1, f32[4,16,64,128]{3,2,1,0:T(8,128)S(1)} %copy-done.10, pred[16,16]{1,0:T(8,128)(4,1)S(1)} %iota_compare_fusion.6), kind=kOutput, calls=%fused_computation.136 | convolution fusion | flops 50337664 | bytes 4195584 | tf_op jit(solution)/shard_map/transpose(jvp(vmap(kj,jpn->kpn)))/dot_general | solution.py:47
  215.5 5.7 %all-to-all-start.4 = ((f32[16,264,128]{2,1,0:T(8,128)}), f32[16,264,128]{2,1,0:T(8,128)}, u32[]{:S(2)}, u32[]{:S(2)}) async-start(f32[16,264,128]{2,1,0:T(8,128)} %pad_maximum_fusion), calls=%async_computation.4 | async-start | bytes 4325376 | tf_op jit(solution)/shard_map/all_to_all | solution.py:155
  221.3 9.0 %fusion.12 = f32[16,4,8,8,256]{4,3,2,1,0:T(8,128)S(1)} fusion(f32[16,4,64,256]{3,2,1,0:T(8,128)} %get-tuple-element.40, f32[4,16,256]{2,0,1:T(4,128)S(1)} %copy.72, bf16[4,8,16,8,256]{4,3,2,1,0:T(8,128)(2,1)S(1)} %bitcast.182, f32[4,16,256,256]{3,2,1,0:T(8,128)} %get-tuple-element.24), kind=kOutput, calls=%fused_computation.21 | convolution fusion | flops 1612709888 | bytes 27328512 | tf_op jit(solution)/shard_map/transpose(jvp(vmap(kij,kjp->kip)))/dot_general | solution.py:35
  234.3 36.7 %all-to-all-done.4 = f32[16,264,128]{2,1,0:T(8,128)} async-done(((f32[16,264,128]{2,1,0:T(8,128)}), f32[16,264,128]{2,1,0:T(8,128)}, u32[]{:S(2)}, u32[]{:S(2)}) %all-to-all-start.4) | async-done | bytes 2162720 | tf_op jit(solution)/shard_map/all_to_all | solution.py:155
  271.0 5.7 %all-to-all-start.2 = ((bf16[16,256,256]{1,2,0:T(8,128)(2,1)}), bf16[16,256,256]{1,2,0:T(8,128)(2,1)S(1)}, u32[]{:S(2)}, u32[]{:S(2)}) async-start(bf16[16,256,256]{1,2,0:T(8,128)(2,1)} %copy.82), calls=%async_computation.2 | async-start | bytes 4194304 | tf_op jit(solution)/shard_map/all_to_all | solution.py:139
  278.4 46.1 %all-to-all-done.2 = bf16[16,256,256]{1,2,0:T(8,128)(2,1)S(1)} async-done(((bf16[16,256,256]{1,2,0:T(8,128)(2,1)}), bf16[16,256,256]{1,2,0:T(8,128)(2,1)S(1)}, u32[]{:S(2)}, u32[]{:S(2)}) %all-to-all-start.2) | async-done | bytes 2097184 | tf_op jit(solution)/shard_map/all_to_all | solution.py:139
  (119 shorter events, 55.1 us)
Async XLA Ops:
  2.0 12.4 %all-to-all-start.1 = ((bf16[256,16,4]{0,2,1:T(4,128)(2,1)}), bf16[256,16,4]{0,2,1:T(4,128)(2,1)S(1)}, u32[]{:S(2)}, u32[]{:S(2)}) async-start(bf16[256,16,4]{0,2,1:T(4,128)(2,1)} %reshape.136), calls=%async_computation.1 | async-start | bytes 65536 | tf_op jit(solution)/shard_map/all_to_all | solution.py:132
  14.4 6.0 %copy-start.15 = (bf16[256,128]{1,0:T(8,128)(2,1)S(1)}, bf16[256,128]{1,0:T(8,128)(2,1)}, u32[]{:S(2)}) copy-start(bf16[256,128]{1,0:T(8,128)(2,1)} %param.8) | copy-start | bytes 196612
  14.4 6.0 %copy-start.16 = (bf16[256,128]{1,0:T(8,128)(2,1)S(1)}, bf16[256,128]{1,0:T(8,128)(2,1)}, u32[]{:S(2)}) copy-start(bf16[256,128]{1,0:T(8,128)(2,1)} %param.9) | copy-start | bytes 196612
  14.4 75.7 %all-to-all-start.3 = ((bf16[256,16,256]{0,2,1:T(8,128)(2,1)}), bf16[256,16,256]{0,2,1:T(8,128)(2,1)S(1)}, u32[]{:S(2)}, u32[]{:S(2)}) async-start(bf16[256,16,256]{0,2,1:T(8,128)(2,1)} %bitcast.189), calls=%async_computation.3 | async-start | bytes 4194304 | tf_op jit(solution)/shard_map/all_to_all | solution.py:130
  20.4 8.2 %collective-permute-start = (bf16[256,128]{1,0:T(8,128)(2,1)S(1)}, bf16[256,128]{1,0:T(8,128)(2,1)S(1)}, u32[]{:S(2)}, u32[]{:S(2)}) collective-permute-start(bf16[256,128]{1,0:T(8,128)(2,1)S(1)} %broadcast_select_fusion.6), channel_id=1, source_target_pairs={{0,2},{2,0},{4,6},{6,4},{8,10},{10,8},{12,14},{14,12},{16,18},{18,... | collective-permute-start | bytes 196616 | tf_op jit(solution)/shard_map/ppermute | solution.py:90
  28.7 5.8 %collective-permute-start.1 = (bf16[512,128]{1,0:T(8,128)(2,1)S(1)}, bf16[512,128]{1,0:T(8,128)(2,1)S(1)}, u32[]{:S(2)}, u32[]{:S(2)}) collective-permute-start(bf16[512,128]{1,0:T(8,128)(2,1)S(1)} %maximum_select_fusion.3), channel_id=1, source_target_pairs={{0,4},{2,6},{4,0},{6,2},{8,12},{10,14},{12,8},{14,10},{16,20},{18,... | collective-permute-start | bytes 393224 | tf_op jit(solution)/shard_map/ppermute | solution.py:90
  34.5 25.5 %collective-permute-start.2 = (bf16[1024,128]{1,0:T(8,128)(2,1)S(1)}, bf16[1024,128]{1,0:T(8,128)(2,1)S(1)}, u32[]{:S(2)}, u32[]{:S(2)}) collective-permute-start(bf16[1024,128]{1,0:T(8,128)(2,1)S(1)} %maximum_select_fusion.2), channel_id=1, source_target_pairs={{0,8},{2,10},{4,12},{6,14},{8,0},{10,2},{12,4},{14,6},{16,24},{18,... | collective-permute-start | bytes 786440 | tf_op jit(solution)/shard_map/ppermute | solution.py:90
  60.2 7.7 %copy-start.14 = (bf16[2048,128]{1,0:T(8,128)(2,1)}, bf16[2048,128]{1,0:T(8,128)(2,1)S(1)}, u32[]{:S(2)}) copy-start(bf16[2048,128]{1,0:T(8,128)(2,1)S(1)} %maximum_select_fusion.1) | copy-start | bytes 1572868
  60.2 28.0 %collective-permute-start.3 = (bf16[2048,128]{1,0:T(8,128)(2,1)S(1)}, bf16[2048,128]{1,0:T(8,128)(2,1)}, u32[]{:S(2)}, u32[]{:S(2)}) collective-permute-start(bf16[2048,128]{1,0:T(8,128)(2,1)S(1)} %maximum_select_fusion.1), channel_id=1, source_target_pairs={{0,16},{2,18},{4,20},{6,22},{8,24},{10,26},{12,28},{14,30},{16,0},... | collective-permute-start | bytes 1572872 | tf_op jit(solution)/shard_map/ppermute | solution.py:90
  90.1 8.4 %copy-start.27 = (f32[64]{0:T(128)S(1)}, f32[64]{0:T(128)}, u32[]{:S(2)}) copy-start(f32[64]{0:T(128)} %param.11) | copy-start | bytes 772
  90.1 8.4 %copy-start.7 = (bf16[256,16,256]{0,2,1:T(8,128)(2,1)}, bf16[256,16,256]{0,2,1:T(8,128)(2,1)S(1)}, u32[]{:S(2)}) copy-start(bf16[256,16,256]{0,2,1:T(8,128)(2,1)S(1)} %all-to-all-done.3) | copy-start | bytes 6291460
  90.1 54.8 %all-to-all-start = ((bf16[256,16,256]{0,2,1:T(8,128)(2,1)}), bf16[256,16,256]{0,2,1:T(8,128)(2,1)}, u32[]{:S(2)}, u32[]{:S(2)}) async-start(bf16[256,16,256]{0,2,1:T(8,128)(2,1)} %bitcast.190), calls=%async_computation | async-start | bytes 4194304 | tf_op jit(solution)/shard_map/all_to_all | solution.py:131
  98.6 2.7 collective-permute-start.4
  99.6 53.6 %copy-start.17 = (f32[4,16,256]{2,1,0:T(8,128)}, f32[4,16,256]{2,1,0:T(8,128)S(1)}, u32[]{:S(2)}) copy-start(f32[4,16,256]{2,1,0:T(8,128)S(1)} %get-tuple-element.36) | copy-start | bytes 196612
  101.5 4.5 %copy-start.5 = (bf16[4096,128]{1,0:T(8,128)(2,1)}, bf16[4096,128]{1,0:T(8,128)(2,1)S(1)}, u32[]{:S(2)}) copy-start(bf16[4096,128]{1,0:T(8,128)(2,1)S(1)} %get-tuple-element.27) | copy-start | bytes 3145732
  199.3 4.4 %copy-start.11 = (f32[16,256,128,1]{2,1,3,0:T(8,128)S(1)}, f32[16,256,128,1]{2,1,3,0:T(8,128)}, u32[]{:S(2)}) copy-start(f32[16,256,128,1]{2,1,3,0:T(8,128)} %fusion.9) | copy-start | bytes 6291460
  207.5 4.1 %copy-start.21 = (f32[4,16,256]{2,1,0:T(8,128)S(1)}, f32[4,16,256]{2,1,0:T(8,128)}, u32[]{:S(2)}) copy-start(f32[4,16,256]{2,1,0:T(8,128)} %get-tuple-element.19) | copy-start | bytes 196612
  207.5 4.4 %copy-start.26 = (f32[4]{0:T(128)S(1)}, f32[4]{0:T(128)}, u32[]{:S(2)}) copy-start(f32[4]{0:T(128)} %copy-done.25) | copy-start | bytes 52
  207.6 4.6 %collective-permute-start.5 = (f32[4096,128]{1,0:T(8,128)}, f32[4096,128]{1,0:T(8,128)}, u32[]{:S(2)}, u32[]{:S(2)}) collective-permute-start(f32[4096,128]{1,0:T(8,128)} %bitcast.34), channel_id=1, source_target_pairs={{0,1},{1,0},{2,3},{3,2},{4,5},{5,4},{6,7},{7,6},{8,9},{9,8},{10,11... | collective-permute-start | bytes 6291464 | tf_op jit(solution)/shard_map/ppermute | solution.py:150
  215.5 5.7 %copy-start.28 = (f32[64]{0:T(128)S(1)}, f32[64]{0:T(128)}, u32[]{:S(2)}) copy-start(f32[64]{0:T(128)} %param.12) | copy-start | bytes 772
  215.5 5.8 %copy-start.3 = (bf16[4096,4,64]{0,2,1:T(8,128)(2,1)S(1)}, bf16[4096,4,64]{0,2,1:T(8,128)(2,1)}, u32[]{:S(2)}) copy-start(bf16[4096,4,64]{0,2,1:T(8,128)(2,1)} %reshape.135) | copy-start | bytes 6291460
  215.5 55.5 %all-to-all-start.4 = ((f32[16,264,128]{2,1,0:T(8,128)}), f32[16,264,128]{2,1,0:T(8,128)}, u32[]{:S(2)}, u32[]{:S(2)}) async-start(f32[16,264,128]{2,1,0:T(8,128)} %pad_maximum_fusion), calls=%async_computation.4 | async-start | bytes 4325376 | tf_op jit(solution)/shard_map/all_to_all | solution.py:155
  271.0 53.6 %all-to-all-start.2 = ((bf16[16,256,256]{1,2,0:T(8,128)(2,1)}), bf16[16,256,256]{1,2,0:T(8,128)(2,1)S(1)}, u32[]{:S(2)}, u32[]{:S(2)}) async-start(bf16[16,256,256]{1,2,0:T(8,128)(2,1)} %copy.82), calls=%async_computation.2 | async-start | bytes 4194304 | tf_op jit(solution)/shard_map/all_to_all | solution.py:139
  278.4 50.5 %collective-permute-start.6 = (f32[256,128]{1,0:T(8,128)S(1)}, f32[256,128]{1,0:T(8,128)S(1)}, u32[]{:S(2)}, u32[]{:S(2)}) collective-permute-start(f32[256,128]{1,0:T(8,128)S(1)} %slice_reduce_fusion), channel_id=1, source_target_pairs={{0,1},{1,0},{2,3},{3,2},{4,5},{5,4},{6,7},{7,6},{8,9},{9,8},{10,11... | collective-permute-start | bytes 393224 | tf_op jit(solution)/shard_map/ppermute | solution.py:163
  (18 other events, 56.7 us)

commit v4 on v3

--- a/solution.py
+++ b/solution.py
@@ -135,13 +135,10 @@
         x_back, raw_back, gb, gc = chunk_backward(
             x_seq, g_seq, raw_seq, b_rows, c_rows, rate_own[sl], gain_own[sl]
         )
-        x_parts.append(
-            lax.all_to_all(x_back, "ctx", split_axis=0, concat_axis=1, tiled=True).reshape(rows, owners, 1, width)
-        )
+        x_parts.append(x_back)
         raw_parts.append(raw_back)
         grad_b_all = gb if grad_b_all is None else grad_b_all + gb
         grad_c_all = gc if grad_c_all is None else grad_c_all + gc
-    grad_x = jnp.concatenate(x_parts, axis=2).reshape(rows, owners * per_owner * head_width)
     raw_all = jnp.concatenate(raw_parts, axis=1)
 
     is_first = half == 0
@@ -160,6 +157,13 @@
         mine = parts.sum(axis=0)
         got_dt = lax.all_to_all(steps_back, "ctx", split_axis=0, concat_axis=0, tiled=True)
     grad_dt = got_dt.transpose(2, 0, 1).reshape(rows, heads_here).astype(jnp.bfloat16)
+    sent = []
+    for part in x_parts:
+        part, _ = lax.optimization_barrier((part, parts))
+        sent.append(
+            lax.all_to_all(part, "ctx", split_axis=0, concat_axis=1, tiled=True).reshape(rows, owners, 1, -1)
+        )
+    grad_x = jnp.concatenate(sent, axis=2).reshape(rows, owners * per_owner * head_width)
     other = lax.ppermute(mine, "tp", [(0, 1), (1, 0)])
     grad_b = jnp.where(is_first, mine, other)
     grad_c = jnp.where(is_first, other, mine)

time: 333 us -> 338 us (1.015)
  local copies, waits for them, and re-layouts: 37.9 us -> 42.9 us
    optimization_barrier x0 -> x1, local copies, waits for them, and re-layouts: none -> 4.09 us  [local(): part, _ = lax.optimization_barrier((part, parts))]
    unnamed x67 -> x66, local copies, waits for them, and re-layouts: 14.5 us -> 15.1 us
  transfers between devices with their start and end apart: 12 -> 12, of which waited for: 9 -> 9; matrix products, arithmetic and copies ran while one was open for 14% -> 13% of each run, Pallas kernels for 0% -> 0%
where the time goes in v4:
time: 338 us; the launch traced here: 335 us
  waiting for transfers between devices  173 us (51%)
  matrix products  66.1 us (20%)
  local copies, waits for them, and re-layouts  42.9 us (13%)
  starting transfers between devices  40.8 us (12%)
  other arithmetic  11.2 us (3%)
    ppermute x4, waiting for transfers between devices, gather_ctx(): theirs = lax.ppermute(have, 'ctx', [(k, k ^ step) for k in range(owners)])  54.9 us
    all_to_all x1, waiting for transfers between devices, local(): lax.all_to_all(part, 'ctx', split_axis=0, concat_axis=1, tiled=True)  43.9 us
    all_to_all x1, waiting for transfers between devices, local(): lax.all_to_all(packed, 'ctx', split_axis=0, concat_axis=0, tiled=True)  38.2 us
    all_to_all x1, waiting for transfers between devices, local(): lax.all_to_all(g_in, 'ctx', split_axis=1, concat_axis=0, tiled=True)  33.6 us
    dot_general x2, matrix products, head_forward(): output = jnp.einsum('kij,kjp->kip', scores, x_blocks, precision=precise)  25.4 us
    unnamed x66, local copies, waits for them, and re-layouts  15.1 us
    dot_general x2, matrix products, head_forward(): jnp.einsum('kin,kpn->kip', reading, entering, precision=precise)  11 us
    dot_general x3, matrix products, head_forward(): states = jnp.einsum('kjp,kjn->kpn', weighted, b_blocks, precision=precise)  10.5 us
  transfers between devices with their start and end apart: 12, of which 9 were waited for; matrix products, arithmetic and copies ran while one was open for 13% of the time, Pallas kernels for 0%

profile of v4, /device:TPU:12, one launch (start us, length us, event | category | flops | bytes accessed | tf_op | source)
XLA Modules:
  0.0 334.8 jit_solution(14153087377416893089)
XLA Ops:
  2.0 7.2 %all-to-all-start.1 = ((bf16[256,16,4]{0,2,1:T(4,128)(2,1)}), bf16[256,16,4]{0,2,1:T(4,128)(2,1)S(1)}, u32[]{:S(2)}, u32[]{:S(2)}) async-start(bf16[256,16,4]{0,2,1:T(4,128)(2,1)} %reshape.135), calls=%async_computation.1 | async-start | bytes 65536 | tf_op jit(solution)/shard_map/all_to_all | solution.py:132
  9.2 4.1 %copy.84 = bf16[256,4096]{0,1:T(8,128)(2,1)} copy(bf16[256,4096]{1,0:T(8,128)(2,1)} %param.7) | data formatting | bytes 4194304 | tf_op args[0]
  14.4 5.9 %all-to-all-start.2 = ((bf16[256,16,256]{0,2,1:T(8,128)(2,1)}), bf16[256,16,256]{0,2,1:T(8,128)(2,1)S(1)}, u32[]{:S(2)}, u32[]{:S(2)}) async-start(bf16[256,16,256]{0,2,1:T(8,128)(2,1)} %bitcast.186), calls=%async_computation.2 | async-start | bytes 4194304 | tf_op jit(solution)/shard_map/all_to_all | solution.py:130
  21.9 6.7 %collective-permute-done = bf16[256,128]{1,0:T(8,128)(2,1)S(1)} collective-permute-done((bf16[256,128]{1,0:T(8,128)(2,1)S(1)}, bf16[256,128]{1,0:T(8,128)(2,1)S(1)}, u32[]{:S(2)}, u32[]{:S(2)}) %collective-permute-start) | collective-permute-done | bytes 65568 | tf_op jit(solution)/shard_map/ppermute | solution.py:90
  29.5 4.9 %collective-permute-done.1 = bf16[512,128]{1,0:T(8,128)(2,1)S(1)} collective-permute-done((bf16[512,128]{1,0:T(8,128)(2,1)S(1)}, bf16[512,128]{1,0:T(8,128)(2,1)S(1)}, u32[]{:S(2)}, u32[]{:S(2)}) %collective-permute-start.1) | collective-permute-done | bytes 131104 | tf_op jit(solution)/shard_map/ppermute | solution.py:90
  37.2 22.8 %collective-permute-done.2 = bf16[1024,128]{1,0:T(8,128)(2,1)S(1)} collective-permute-done((bf16[1024,128]{1,0:T(8,128)(2,1)S(1)}, bf16[1024,128]{1,0:T(8,128)(2,1)S(1)}, u32[]{:S(2)}, u32[]{:S(2)}) %collective-permute-start.2) | collective-permute-done | bytes 262176 | tf_op jit(solution)/shard_map/ppermute | solution.py:90
  63.7 4.1 %copy.72 = bf16[256,4096]{0,1:T(8,128)(2,1)} copy(bf16[256,4096]{1,0:T(8,128)(2,1)} %param.13) | data formatting | bytes 4194304 | tf_op args[6]
  67.8 20.4 %collective-permute-done.3 = bf16[2048,128]{1,0:T(8,128)(2,1)} collective-permute-done((bf16[2048,128]{1,0:T(8,128)(2,1)S(1)}, bf16[2048,128]{1,0:T(8,128)(2,1)}, u32[]{:S(2)}, u32[]{:S(2)}) %collective-permute-start.3) | collective-permute-done | bytes 524320 | tf_op jit(solution)/shard_map/ppermute | solution.py:90
  90.1 8.0 %all-to-all-start = ((bf16[256,16,256]{0,2,1:T(8,128)(2,1)}), bf16[256,16,256]{0,2,1:T(8,128)(2,1)}, u32[]{:S(2)}, u32[]{:S(2)}) async-start(bf16[256,16,256]{0,2,1:T(8,128)(2,1)} %bitcast.187), calls=%async_computation | async-start | bytes 4194304 | tf_op jit(solution)/shard_map/all_to_all | solution.py:131
  111.0 33.6 %all-to-all-done = bf16[256,16,256]{0,2,1:T(8,128)(2,1)} async-done(((bf16[256,16,256]{0,2,1:T(8,128)(2,1)}), bf16[256,16,256]{0,2,1:T(8,128)(2,1)}, u32[]{:S(2)}, u32[]{:S(2)}) %all-to-all-start) | async-done | bytes 2097184 | tf_op jit(solution)/shard_map/all_to_all | solution.py:131
  144.6 4.1 %copy.73 = bf16[16,256,1,256]{1,0,3,2:T(8,128)(2,1)} copy(bf16[16,256,1,256]{1,3,0,2:T(8,128)(2,1)} %bitcast.2) | data formatting | bytes 4194304 | tf_op jit(solution)/shard_map/all_to_all | solution.py:131
  148.7 4.2 %reshape.134 = bf16[4096,4,64]{0,2,1:T(8,128)(2,1)} reshape(bf16[16,256,1,256]{1,0,3,2:T(8,128)(2,1)} %copy.73) | data formatting | bytes 4194304 | tf_op jit(solution)/shard_map/reshape | solution.py:131
  152.9 5.9 %multiply_reduce_fusion.4 = (f32[4,16]{1,0:T(4,128)}, f32[4,16,64,128]{3,2,1,0:T(8,128)S(1)}) fusion(f32[16,256,128]{1,2,0:T(8,128)} %copy.75, f32[4,16,256]{2,1,0:T(8,128)S(1)} %get-tuple-element.38, bf16[4,8,16,8,256]{4,3,2,1,0:T(8,128)(2,1)} %bitcast.176), kind=kOutput, calls=%fused_computation.42 | convolution fusion | flops 808452032 | bytes 6357248 | tf_op jit(solution)/shard_map/transpose(jvp(vmap(kin,kpn->kip)))/dot_general | solution.py:51
  160.8 4.0 %fusion.10 = (f32[4,16,256]{2,0,1:T(4,128)S(1)}, f32[16,4,64,256]{3,2,1,0:T(8,128)}) fusion(bf16[4,8,16,8,256]{4,3,2,1,0:T(8,128)(2,1)S(1)} %bitcast.168, bf16[16,256,128,1]{2,1,3,0:T(8,128)(2,1)S(1)} %bitcast.173, f32[16,4,64,128]{3,0,2,1:T(8,128)S(1)} %fusion.44), kind=kOutput, calls=%fused_computation.18 | convolution fusion | flops 808435712 | bytes 9502720 | tf_op jit(solution)/shard_map/transpose(jvp(vmap(kjp,kjn->kpn)))/dot_general | solution.py:38
  164.8 16.4 %fusion.5 = (f32[4,16,256]{2,1,0:T(8,128)}, f32[4,16,256]{2,1,0:T(8,128)}, f32[4,16,256]{2,1,0:T(8,128)S(1)}, f32[16,256,256]{2,1,0:T(8,128)}, f32[4,16,256,256]{3,2,1,0:T(8,128)}) fusion(f32[4,16,256]{2,1,0:T(8,128)S(1)} %bitcast.202, f32[4,16,256]{2,1,0:T(8,128)S(1)} %get-tuple-element.39, f32[16,256,256]{2,1,0:T(8,128)S(1)} %copy-done.12, ...), kind=kOutput, calls=%fused_computation.9 | convolution fusion | flops 594493440 | bytes 29753344 | tf_op jit(solution)/shard_map/transpose(jvp(vmap(kij,kjp->kip)))/dot_general | solution.py:35
  182.0 5.2 %fusion.9 = f32[16,256,128,1]{2,1,3,0:T(8,128)} fusion(f32[4,16,256]{2,0,1:T(4,128)S(1)} %copy.74, f32[16,4,64,128]{3,0,2,1:T(8,128)S(1)} %fusion.44, bf16[4,8,16,8,256]{4,3,2,1,0:T(8,128)(2,1)S(1)} %bitcast.170), kind=kOutput, calls=%fused_computation.17 | convolution fusion | flops 807403520 | bytes 6356992 | tf_op jit(solution)/shard_map/transpose(jvp(vmap(kjp,kjn->kpn)))/dot_general | solution.py:38
  191.9 5.1 %multiply_reduce_fusion.3 = (f32[16,256,128]{1,2,0:T(8,128)}, f32[4,16,256]{2,1,0:T(8,128)}) fusion(f32[4,16,256]{2,1,0:T(8,128)S(1)} %copy-done.18, f32[16,256,128]{1,2,0:T(8,128)S(1)} %copy-done.13, f32[4,16,64,128]{3,1,2,0:T(8,128)S(1)} %fusion.47, bf16[4,8,16,8,256]{4,3,2,1,0:T(8,128)(2,1)S(1)} %bitcast.178), kind=kOutput, calls=%fused_computation.11 | convolution fusion | flops 813154304 | bytes 8519680 | tf_op jit(solution)/shard_map/transpose(jvp(vmap(kin,kpn->kip)))/dot_general | solution.py:51
  215.3 5.3 %all-to-all-start.3 = ((f32[16,264,128]{2,1,0:T(8,128)}), f32[16,264,128]{2,1,0:T(8,128)}, u32[]{:S(2)}, u32[]{:S(2)}) async-start(f32[16,264,128]{2,1,0:T(8,128)} %pad_maximum_fusion), calls=%async_computation.3 | async-start | bytes 4325376 | tf_op jit(solution)/shard_map/all_to_all | solution.py:152
  220.7 9.0 %fusion.12 = f32[16,4,8,8,256]{4,3,2,1,0:T(8,128)S(1)} fusion(f32[16,4,64,256]{3,2,1,0:T(8,128)} %get-tuple-element.42, f32[4,16,256]{2,0,1:T(4,128)S(1)} %copy.74, bf16[4,8,16,8,256]{4,3,2,1,0:T(8,128)(2,1)S(1)} %bitcast.179, f32[4,16,256,256]{3,2,1,0:T(8,128)} %get-tuple-element.26), kind=kOutput, calls=%fused_computation.21 | convolution fusion | flops 1612709888 | bytes 27328512 | tf_op jit(solution)/shard_map/transpose(jvp(vmap(kij,kjp->kip)))/dot_general | solution.py:35
  232.4 38.2 %all-to-all-done.3 = f32[16,264,128]{2,1,0:T(8,128)} async-done(((f32[16,264,128]{2,1,0:T(8,128)}), f32[16,264,128]{2,1,0:T(8,128)}, u32[]{:S(2)}, u32[]{:S(2)}) %all-to-all-start.3) | async-done | bytes 2162720 | tf_op jit(solution)/shard_map/all_to_all | solution.py:152
  270.6 4.1 %copy.100 = bf16[4096,256]{1,0:T(8,128)(2,1)} copy(bf16[4096,256]{0,1:T(8,128)(2,1)} %bitcast.191) | data formatting | bytes 4194304 | tf_op jit(solution)/shard_map/optimization_barrier | solution.py:162
  274.7 5.6 %all-to-all-start.4 = ((bf16[16,256,256]{2,1,0:T(8,128)(2,1)}), bf16[16,256,256]{2,1,0:T(8,128)(2,1)S(1)}, u32[]{:S(2)}, u32[]{:S(2)}) async-start(bf16[16,256,256]{2,1,0:T(8,128)(2,1)} %bitcast.189), calls=%async_computation.4 | async-start | bytes 4194304 | tf_op jit(solution)/shard_map/all_to_all | solution.py:164
  284.3 43.9 %all-to-all-done.4 = bf16[16,256,256]{2,1,0:T(8,128)(2,1)S(1)} async-done(((bf16[16,256,256]{2,1,0:T(8,128)(2,1)}), bf16[16,256,256]{2,1,0:T(8,128)(2,1)S(1)}, u32[]{:S(2)}, u32[]{:S(2)}) %all-to-all-start.4) | async-done | bytes 2097184 | tf_op jit(solution)/shard_map/all_to_all | solution.py:164
  330.6 4.1 %copy.102 = bf16[256,4096]{1,0:T(8,128)(2,1)} copy(bf16[256,4096]{0,1:T(8,128)(2,1)} %bitcast.190) | data formatting | bytes 4194304
  (119 shorter events, 60.7 us)
Async XLA Ops:
  2.0 12.4 %all-to-all-start.1 = ((bf16[256,16,4]{0,2,1:T(4,128)(2,1)}), bf16[256,16,4]{0,2,1:T(4,128)(2,1)S(1)}, u32[]{:S(2)}, u32[]{:S(2)}) async-start(bf16[256,16,4]{0,2,1:T(4,128)(2,1)} %reshape.135), calls=%async_computation.1 | async-start | bytes 65536 | tf_op jit(solution)/shard_map/all_to_all | solution.py:132
  14.4 6.0 %copy-start.15 = (bf16[256,128]{1,0:T(8,128)(2,1)S(1)}, bf16[256,128]{1,0:T(8,128)(2,1)}, u32[]{:S(2)}) copy-start(bf16[256,128]{1,0:T(8,128)(2,1)} %param.8) | copy-start | bytes 196612
  14.4 6.0 %copy-start.16 = (bf16[256,128]{1,0:T(8,128)(2,1)S(1)}, bf16[256,128]{1,0:T(8,128)(2,1)}, u32[]{:S(2)}) copy-start(bf16[256,128]{1,0:T(8,128)(2,1)} %param.9) | copy-start | bytes 196612
  14.4 75.7 %all-to-all-start.2 = ((bf16[256,16,256]{0,2,1:T(8,128)(2,1)}), bf16[256,16,256]{0,2,1:T(8,128)(2,1)S(1)}, u32[]{:S(2)}, u32[]{:S(2)}) async-start(bf16[256,16,256]{0,2,1:T(8,128)(2,1)} %bitcast.186), calls=%async_computation.2 | async-start | bytes 4194304 | tf_op jit(solution)/shard_map/all_to_all | solution.py:130
  20.4 8.2 %collective-permute-start = (bf16[256,128]{1,0:T(8,128)(2,1)S(1)}, bf16[256,128]{1,0:T(8,128)(2,1)S(1)}, u32[]{:S(2)}, u32[]{:S(2)}) collective-permute-start(bf16[256,128]{1,0:T(8,128)(2,1)S(1)} %broadcast_select_fusion.6), channel_id=1, source_target_pairs={{0,2},{2,0},{4,6},{6,4},{8,10},{10,8},{12,14},{14,12},{16,18},{18,... | collective-permute-start | bytes 196616 | tf_op jit(solution)/shard_map/ppermute | solution.py:90
  28.7 5.8 %collective-permute-start.1 = (bf16[512,128]{1,0:T(8,128)(2,1)S(1)}, bf16[512,128]{1,0:T(8,128)(2,1)S(1)}, u32[]{:S(2)}, u32[]{:S(2)}) collective-permute-start(bf16[512,128]{1,0:T(8,128)(2,1)S(1)} %maximum_select_fusion.3), channel_id=1, source_target_pairs={{0,4},{2,6},{4,0},{6,2},{8,12},{10,14},{12,8},{14,10},{16,20},{18,... | collective-permute-start | bytes 393224 | tf_op jit(solution)/shard_map/ppermute | solution.py:90
  34.5 25.5 %collective-permute-start.2 = (bf16[1024,128]{1,0:T(8,128)(2,1)S(1)}, bf16[1024,128]{1,0:T(8,128)(2,1)S(1)}, u32[]{:S(2)}, u32[]{:S(2)}) collective-permute-start(bf16[1024,128]{1,0:T(8,128)(2,1)S(1)} %maximum_select_fusion.2), channel_id=1, source_target_pairs={{0,8},{2,10},{4,12},{6,14},{8,0},{10,2},{12,4},{14,6},{16,24},{18,... | collective-permute-start | bytes 786440 | tf_op jit(solution)/shard_map/ppermute | solution.py:90
  60.2 7.7 %copy-start.14 = (bf16[2048,128]{1,0:T(8,128)(2,1)}, bf16[2048,128]{1,0:T(8,128)(2,1)S(1)}, u32[]{:S(2)}) copy-start(bf16[2048,128]{1,0:T(8,128)(2,1)S(1)} %maximum_select_fusion.1) | copy-start | bytes 1572868
  60.2 28.0 %collective-permute-start.3 = (bf16[2048,128]{1,0:T(8,128)(2,1)S(1)}, bf16[2048,128]{1,0:T(8,128)(2,1)}, u32[]{:S(2)}, u32[]{:S(2)}) collective-permute-start(bf16[2048,128]{1,0:T(8,128)(2,1)S(1)} %maximum_select_fusion.1), channel_id=1, source_target_pairs={{0,16},{2,18},{4,20},{6,22},{8,24},{10,26},{12,28},{14,30},{16,0},... | collective-permute-start | bytes 1572872 | tf_op jit(solution)/shard_map/ppermute | solution.py:90
  90.1 8.0 %copy-start.27 = (f32[64]{0:T(128)S(1)}, f32[64]{0:T(128)}, u32[]{:S(2)}) copy-start(f32[64]{0:T(128)} %param.11) | copy-start | bytes 772
  90.1 8.0 %copy-start.7 = (bf16[256,16,256]{0,2,1:T(8,128)(2,1)}, bf16[256,16,256]{0,2,1:T(8,128)(2,1)S(1)}, u32[]{:S(2)}) copy-start(bf16[256,16,256]{0,2,1:T(8,128)(2,1)S(1)} %all-to-all-done.2) | copy-start | bytes 6291460
  90.1 54.5 %all-to-all-start = ((bf16[256,16,256]{0,2,1:T(8,128)(2,1)}), bf16[256,16,256]{0,2,1:T(8,128)(2,1)}, u32[]{:S(2)}, u32[]{:S(2)}) async-start(bf16[256,16,256]{0,2,1:T(8,128)(2,1)} %bitcast.187), calls=%async_computation | async-start | bytes 4194304 | tf_op jit(solution)/shard_map/all_to_all | solution.py:131
  98.2 2.7 collective-permute-start.4
  99.3 53.6 %copy-start.17 = (f32[4,16,256]{2,1,0:T(8,128)}, f32[4,16,256]{2,1,0:T(8,128)S(1)}, u32[]{:S(2)}) copy-start(f32[4,16,256]{2,1,0:T(8,128)S(1)} %get-tuple-element.38) | copy-start | bytes 196612
  101.1 4.5 %copy-start.5 = (bf16[4096,128]{1,0:T(8,128)(2,1)}, bf16[4096,128]{1,0:T(8,128)(2,1)S(1)}, u32[]{:S(2)}) copy-start(bf16[4096,128]{1,0:T(8,128)(2,1)S(1)} %get-tuple-element.29) | copy-start | bytes 3145732
  199.2 4.4 %copy-start.11 = (f32[16,256,128,1]{2,1,3,0:T(8,128)S(1)}, f32[16,256,128,1]{2,1,3,0:T(8,128)}, u32[]{:S(2)}) copy-start(f32[16,256,128,1]{2,1,3,0:T(8,128)} %fusion.9) | copy-start | bytes 6291460
  207.4 4.1 %copy-start.21 = (f32[4,16,256]{2,1,0:T(8,128)S(1)}, f32[4,16,256]{2,1,0:T(8,128)}, u32[]{:S(2)}) copy-start(f32[4,16,256]{2,1,0:T(8,128)} %get-tuple-element.21) | copy-start | bytes 196612
  207.4 4.4 %copy-start.26 = (f32[4]{0:T(128)S(1)}, f32[4]{0:T(128)}, u32[]{:S(2)}) copy-start(f32[4]{0:T(128)} %copy-done.25) | copy-start | bytes 52
  207.4 4.6 %collective-permute-start.5 = (f32[4096,128]{1,0:T(8,128)}, f32[4096,128]{1,0:T(8,128)}, u32[]{:S(2)}, u32[]{:S(2)}) collective-permute-start(f32[4096,128]{1,0:T(8,128)} %bitcast.33), channel_id=1, source_target_pairs={{0,1},{1,0},{2,3},{3,2},{4,5},{5,4},{6,7},{7,6},{8,9},{9,8},{10,11... | collective-permute-start | bytes 6291464 | tf_op jit(solution)/shard_map/ppermute | solution.py:147
  215.3 5.3 %copy-start.28 = (f32[64]{0:T(128)S(1)}, f32[64]{0:T(128)}, u32[]{:S(2)}) copy-start(f32[64]{0:T(128)} %param.12) | copy-start | bytes 772
  215.3 5.4 %copy-start.3 = (bf16[4096,4,64]{0,2,1:T(8,128)(2,1)S(1)}, bf16[4096,4,64]{0,2,1:T(8,128)(2,1)}, u32[]{:S(2)}) copy-start(bf16[4096,4,64]{0,2,1:T(8,128)(2,1)} %reshape.134) | copy-start | bytes 6291460
  215.3 55.3 %all-to-all-start.3 = ((f32[16,264,128]{2,1,0:T(8,128)}), f32[16,264,128]{2,1,0:T(8,128)}, u32[]{:S(2)}, u32[]{:S(2)}) async-start(f32[16,264,128]{2,1,0:T(8,128)} %pad_maximum_fusion), calls=%async_computation.3 | async-start | bytes 4325376 | tf_op jit(solution)/shard_map/all_to_all | solution.py:152
  274.7 53.5 %all-to-all-start.4 = ((bf16[16,256,256]{2,1,0:T(8,128)(2,1)}), bf16[16,256,256]{2,1,0:T(8,128)(2,1)S(1)}, u32[]{:S(2)}, u32[]{:S(2)}) async-start(bf16[16,256,256]{2,1,0:T(8,128)(2,1)} %bitcast.189), calls=%async_computation.4 | async-start | bytes 4194304 | tf_op jit(solution)/shard_map/all_to_all | solution.py:164
  282.0 1.6 collective-permute-start.6
  (18 other events, 56.7 us)
